TPU v7x, 512 devices: a whole 4x8x8 slice. The times are simulated.
512 devices in a mesh: axial: 64 (over y_hi, z, core), circ: 8 (over x, y_lo).
Axes of the slice: x: 4, y: 8 (y_hi: 4, y_lo: 2; y = y_hi * 2 + y_lo), z: 8, core: 2. Of those that a mesh axis runs over, the one named last changes fastest.
Arguments:
- mode_shapes: float32 [128, 16, 128, 512], P('axial', 'circ'), may hold values from -0.03125 to 0.03125
- amplitude: float32 [128, 16, 128], P('axial', 'circ'), may hold values from 0.3 to 3
- pair_list: int32 [64, 8, 3, 20], P('axial', 'circ'), may hold values from -1 to 3, as said below
- pair_counts: int32 [64, 8], P('axial', 'circ'), may hold values from 2 to 20, as said below
Outputs:
- modal_spectrum: float32 [2, 512, 512], P(None, 'axial', 'circ')
Inputs may be any that keep to these rules, and one draw needn't show every extreme that they name: `pair_list`: each device's 20 slots hold distinct pairs, and each of its local blocks is the row block of exactly five slots, one for each of the five offsets. Entry 0 is the row block's local index i * 2 + j of the device's 2 x 2 blocks, entry 1 the axial offset (0 or 1), entry 2 the circumferential offset (-1, 0 or 1), and an axial offset 0 comes only with a circumferential offset of 0 or 1. `pair_counts`: some device keeps all 20 slots.
All inputs are finite; a program needn't handle non-finite values.
Results may differ from a plain program's by a relative error of at most 0.0022.
Values may be sent and summed in bfloat16 or wider, within the bound.
No kernel may reach another device: no remote copies, remote signals or barrier semaphores. Data moves between devices by JAX's collectives and lax.ppermute only.
A program may use at most 64 MiB of HBM per device.

v0:
```python
import jax
import jax.numpy as jnp
from jax import lax
from jax.sharding import PartitionSpec as P

ALONG = 16
AROUND = 8


axial_decay = 0.125
circ_decay = 0.16
wavenumber = 0.6


def with_halo(block, sides, width):
    for axis, dim in sides:
        count = lax.axis_size(axis)
        forward = [(i, i + 1) for i in range(count - 1)]
        forward.append((count - 1, 0))
        backward = [(target, source) for source, target in forward]
        low = lax.ppermute(
            lax.slice_in_dim(block, block.shape[dim] - width, None, axis=dim), axis, forward
        )
        high = lax.ppermute(lax.slice_in_dim(block, 0, width, axis=dim), axis, backward)
        block = jnp.concatenate([low, block, high], axis=dim)
    return block


def from_behind(block, axis, distance):
    devices = range(lax.axis_size(axis))
    route = [(i - distance, i) for i in devices if i - distance in devices]
    return lax.ppermute(block, axis, route)


def in_blocks(shard, dim, length):
    dims = shard.shape
    blocks = shard.reshape(*dims[:dim], length, dims[dim] // length, *dims[dim + 1 :])
    return jnp.moveaxis(blocks, dim, 0)


def sent_and_summed(shard, axis, dim):
    blocks = in_blocks(shard, dim, lax.axis_size(axis))
    arrived = lax.all_to_all(blocks, axis, split_axis=0, concat_axis=0, tiled=True)
    return arrived.sum(axis=0)


def corcos_tiles(step_along, step_around, weight):
    patch_index = jnp.arange(ALONG * AROUND, dtype=jnp.int32)
    along_pos = (patch_index // AROUND).astype(jnp.float32)
    around_pos = (patch_index % AROUND).astype(jnp.float32)
    gap_along = (
        step_along.astype(jnp.float32)[:, None, None] * ALONG
        + along_pos[None, None, :]
        - along_pos[None, :, None]
    )
    gap_around = (
        step_around.astype(jnp.float32)[:, None, None] * AROUND
        + around_pos[None, None, :]
        - around_pos[None, :, None]
    )
    envelope = weight[:, None, None] * jnp.exp(
        -axial_decay * jnp.abs(gap_along) - circ_decay * jnp.abs(gap_around)
    )
    real_tile = envelope * jnp.cos(wavenumber * gap_along)
    imag_tile = -envelope * jnp.sin(wavenumber * gap_along)
    return jnp.stack([real_tile, imag_tile], axis=1).astype(jnp.bfloat16)


def slot_products(chosen, slot_index, pair_total, flattened, around_blocks):
    row_block = chosen[0]
    step_along = chosen[1]
    step_around = chosen[2]
    valid = (slot_index < pair_total).astype(jnp.float32)
    weight = valid * jnp.where((step_along == 0) & (step_around == 0), 0.5, 1.0).astype(jnp.float32)
    column = (
        (row_block // around_blocks + step_along) * (around_blocks + 2)
        + row_block % around_blocks
        + step_around
        + 1
    )
    columns = flattened[column]
    tiles = corcos_tiles(step_along, step_around, weight)
    return jnp.einsum("pcij,pjm->picm", tiles, columns, preferred_element_type=jnp.float32)


def body(mode_shapes, amplitude, pair_list, pair_counts):
    along_blocks, around_blocks, patch_count, mode_count = mode_shapes.shape
    block_count = along_blocks * around_blocks
    weighted = (mode_shapes * amplitude[..., None]).astype(jnp.bfloat16)
    widened = with_halo(weighted, (("circ", 1),), 1)
    ahead_rows = from_behind(widened[:1], "axial", -1)
    extended = jnp.concatenate([widened, ahead_rows], axis=0)
    flattened = extended.reshape((along_blocks + 1) * (around_blocks + 2), patch_count, mode_count)
    listing = pair_list[0, 0]
    pair_total = pair_counts[0, 0]
    slot_total = listing.shape[1]
    group_size = 5 * around_blocks
    group_count = slot_total // group_size
    empty = jnp.zeros((block_count, patch_count, 2 * mode_count), jnp.float32)
    sort_keys = listing[0] * slot_total + jnp.arange(slot_total, dtype=jnp.int32)
    ordering = jnp.argsort(sort_keys)
    ordered = listing[:, ordering]

    def add_row(index, totals):
        chosen = lax.dynamic_slice_in_dim(ordered, index * group_size, group_size, 1)
        slot_index = lax.dynamic_slice_in_dim(ordering, index * group_size, group_size, 0)
        products = slot_products(chosen, slot_index, pair_total, flattened, around_blocks)
        summed = jnp.sum(products.reshape(around_blocks, 5, patch_count, 2 * mode_count), axis=1)
        return lax.dynamic_update_slice_in_dim(totals, summed, index * around_blocks, 0)

    row_sums = lax.fori_loop(0, group_count, add_row, empty)
    rounded = row_sums.astype(jnp.bfloat16).reshape(block_count * patch_count, 2 * mode_count)
    local = weighted.reshape(block_count * patch_count, mode_count)
    cross = lax.dot_general(
        local, rounded, (((0,), (0,)), ((), ())), preferred_element_type=jnp.float32
    )
    real_part = cross[:, :mode_count]
    imag_part = cross[:, mode_count:]
    summand = jnp.stack([real_part + real_part.T, imag_part - imag_part.T])
    partial_value = sent_and_summed(summand, "circ", 2)
    result = sent_and_summed(partial_value, "axial", 1)
    return result


def solution(mesh):
    in_specs = (
        P("axial", "circ", None, None),
        P("axial", "circ", None),
        P("axial", "circ", None, None),
        P("axial", "circ"),
    )
    out_specs = P(None, "axial", "circ")
    return jax.shard_map(body, mesh=mesh, in_specs=in_specs, out_specs=out_specs, check_vma=False)
```

profile of v0, /device:TPU:1, one launch (start us, length us, event | category | flops | bytes accessed | tf_op | source)
XLA Modules:
  0.0 135.2 jit_solution(17313318221329304763)
XLA Ops:
  0.0 1.4 %multiply_convert_fusion = bf16[2,2,128,512]{3,2,1,0:T(8,128)(2,1)S(1)} fusion(f32[2,2,128,512]{3,2,1,0:T(8,128)} %param.6, f32[2,2,128]{2,1,0:T(2,128)} %param.7), kind=kLoop, calls=%fused_computation.52 | loop fusion | flops 524288 | bytes 1574912 | tf_op jit(solution)/shard_map/convert_element_type | solution.py:89
  1.4 4.0 %collective-permute-start = (bf16[2,1,128,512]{3,2,1,0:T(8,128)(2,1)S(1)}, bf16[2,1,128,512]{3,2,1,0:T(8,128)(2,1)S(1)}, u32[]{:S(2)}, u32[]{:S(2)}) collective-permute-start(bf16[2,1,128,512]{3,2,1,0:T(8,128)(2,1)S(1)} %get-tuple-element.247), channel_id=1, source_target_pairs={{0,1},{1,2},{2,3},{3,4},{4,5},{5,6},{6,7},{7,0},{8,9},{9,10},{10,1... | collective-permute-start | bytes 786440 | tf_op jit(solution)/shard_map/ppermute | solution.py:21
  5.5 4.1 %collective-permute-start.1 = (bf16[2,1,128,512]{3,2,1,0:T(8,128)(2,1)S(1)}, bf16[2,1,128,512]{3,2,1,0:T(8,128)(2,1)S(1)}, u32[]{:S(2)}, u32[]{:S(2)}) collective-permute-start(bf16[2,1,128,512]{3,2,1,0:T(8,128)(2,1)S(1)} %get-tuple-element.248), channel_id=1, source_target_pairs={{1,0},{2,1},{3,2},{4,3},{5,4},{6,5},{7,6},{0,7},{9,8},{10,9},{11,1... | collective-permute-start | bytes 786440 | tf_op jit(solution)/shard_map/ppermute | solution.py:24
  9.7 1.7 %collective-permute-done = bf16[2,1,128,512]{3,2,1,0:T(8,128)(2,1)S(1)} collective-permute-done((bf16[2,1,128,512]{3,2,1,0:T(8,128)(2,1)S(1)}, bf16[2,1,128,512]{3,2,1,0:T(8,128)(2,1)S(1)}, u32[]{:S(2)}, u32[]{:S(2)}) %collective-permute-start) | collective-permute-done | bytes 262176 | tf_op jit(solution)/shard_map/ppermute | solution.py:21
  11.4 5.7 %collective-permute-done.1 = bf16[2,1,128,512]{3,2,1,0:T(8,128)(2,1)S(1)} collective-permute-done((bf16[2,1,128,512]{3,2,1,0:T(8,128)(2,1)S(1)}, bf16[2,1,128,512]{3,2,1,0:T(8,128)(2,1)S(1)}, u32[]{:S(2)}, u32[]{:S(2)}) %collective-permute-start.1) | collective-permute-done | bytes 262176 | tf_op jit(solution)/shard_map/ppermute | solution.py:24
  17.2 4.9 %collective-permute-start.2 = (bf16[1,4,128,512]{3,2,1,0:T(8,128)(2,1)S(1)}, bf16[1,4,128,512]{3,2,1,0:T(8,128)(2,1)S(1)}, u32[]{:S(2)}, u32[]{:S(2)}) collective-permute-start(bf16[1,4,128,512]{3,2,1,0:T(8,128)(2,1)S(1)} %pad_maximum_fusion.1), channel_id=1, source_target_pairs={{8,0},{16,8},{24,16},{32,24},{40,32},{48,40},{56,48},{64,56},{72,6... | collective-permute-start | bytes 1572872 | tf_op jit(solution)/shard_map/ppermute | solution.py:32
  22.1 1.6 %sort.17 = (s32[20]{0:T(128)}, s32[20]{0:T(128)S(1)}) sort(s32[20]{0:T(128)S(1)} %bitcast_add_fusion.2, s32[20]{0:T(128)S(1)} %iota.49), dimensions={0}, to_apply=%region_0.0 | sort | flops 100 | bytes 320 | tf_op jit(solution)/shard_map/jit(argsort)/sort | solution.py:101
  24.4 5.8 %collective-permute-done.2 = bf16[1,4,128,512]{3,2,1,0:T(8,128)(2,1)S(1)} collective-permute-done((bf16[1,4,128,512]{3,2,1,0:T(8,128)(2,1)S(1)}, bf16[1,4,128,512]{3,2,1,0:T(8,128)(2,1)S(1)}, u32[]{:S(2)}, u32[]{:S(2)}) %collective-permute-start.2) | collective-permute-done | bytes 524320 | tf_op jit(solution)/shard_map/ppermute | solution.py:32
  31.6 26.6 %while.16 = (s32[]{:T(128)}, bf16[4,128,1024]{2,1,0:T(8,128)(2,1)}, s32[3,20]{1,0:T(4,128)S(1)}, bf16[12,128,512]{2,1,0:T(8,128)(2,1)S(1)}, s32[20]{0:T(128)S(1)...) while((s32[]{:T(128)}, bf16[4,128,1024]{2,1,0:T(8,128)(2,1)}, ...), condition=%wide.region_3.4_spmd, body=%wide.region_1.3_spmd.sunk | while | flops 340203136 | bytes 18378884 | solution.py:111
  32.5 3.5 %fusion.37 = (bf16[10,1,128,128]{3,2,1,0:T(8,128)(2,1)}, bf16[10,1,128,128]{3,2,1,0:T(8,128)(2,1)}) fusion(f32[128]{0:T(128)S(1)} %get-tuple-element.292, f32[10,128]{1,0:T(8,128)S(1)} %broadcast_add_fusion.4, f32[128]{0:T(128)S(1)} %get-tuple-element.294, f32[10,128]{1,0:T(8,128)S(1)} %broadcast_add_fusion.5, f32[10]{0:T(128)S(1)} %compare_select_fusion.7), kind=kLoop, calls=%fused_computation.9.clone.1 | loop fusion | flops 2293760 | bytes 666664 | tf_op jit(solution)/shard_map/convert
  36.7 4.3 %fusion.38 = f32[10,512,2,128]{3,1,2,0:T(8,128)} fusion(bf16[10,128,512]{2,1,0:T(8,128)(2,1)S(1)} %gather_fusion, bf16[10,1,128,128]{3,2,1,0:T(8,128)(2,1)} %get-tuple-element.296, bf16[10,1,128,128]{3,2,1,0:T(8,128)(2,1)} %get-tuple-element.297), kind=kOutput, calls=%fused_computation.2.clone.1 | convolution fusion | flops 336855040 | bytes 7208960 | tf_op jit(solution)/shard_map/while/body/eval_jaxpr/pcij,pjm->picm/dot_general | solution.py:83
  41.0 2.8 %reduce_sum.38 = bf16[2,128,1024]{1,2,0:T(8,128)(2,1)S(1)} reduce(f32[2,5,128,1024]{2,3,1,0:T(8,128)} %bitcast.80, f32[]{:T(128)} %constant.258.clone.1..sunk), dimensions={1}, to_apply=%region_2.2 | reduce | flops 1048576 | bytes 5767172 | tf_op jit(solution)/shard_map/while/body/eval_jaxpr/reduce_sum | solution.py:108
  45.8 3.5 %fusion.37 = (bf16[10,1,128,128]{3,2,1,0:T(8,128)(2,1)}, bf16[10,1,128,128]{3,2,1,0:T(8,128)(2,1)}) fusion(f32[128]{0:T(128)S(1)} %get-tuple-element.292, f32[10,128]{1,0:T(8,128)S(1)} %broadcast_add_fusion.4, f32[128]{0:T(128)S(1)} %get-tuple-element.294, f32[10,128]{1,0:T(8,128)S(1)} %broadcast_add_fusion.5, f32[10]{0:T(128)S(1)} %compare_select_fusion.7), kind=kLoop, calls=%fused_computation.9.clone.1 | loop fusion | flops 2293760 | bytes 666664 | tf_op jit(solution)/shard_map/convert
  50.0 4.3 %fusion.38 = f32[10,512,2,128]{3,1,2,0:T(8,128)} fusion(bf16[10,128,512]{2,1,0:T(8,128)(2,1)S(1)} %gather_fusion, bf16[10,1,128,128]{3,2,1,0:T(8,128)(2,1)} %get-tuple-element.296, bf16[10,1,128,128]{3,2,1,0:T(8,128)(2,1)} %get-tuple-element.297), kind=kOutput, calls=%fused_computation.2.clone.1 | convolution fusion | flops 336855040 | bytes 7208960 | tf_op jit(solution)/shard_map/while/body/eval_jaxpr/pcij,pjm->picm/dot_general | solution.py:83
  54.3 2.8 %reduce_sum.38 = bf16[2,128,1024]{1,2,0:T(8,128)(2,1)S(1)} reduce(f32[2,5,128,1024]{2,3,1,0:T(8,128)} %bitcast.80, f32[]{:T(128)} %constant.258.clone.1..sunk), dimensions={1}, to_apply=%region_2.2 | reduce | flops 1048576 | bytes 5767172 | tf_op jit(solution)/shard_map/while/body/eval_jaxpr/reduce_sum | solution.py:108
  58.1 1.9 %fusion.24 = f32[512,1024]{1,0:T(8,128)S(1)} fusion(bf16[512,512]{1,0:T(8,128)(2,1)S(1)} %bitcast.82, bf16[512,1024]{1,0:T(8,128)(2,1)} %bitcast.83), kind=kOutput, calls=%fused_computation.60 | convolution fusion | flops 536870912 | bytes 3670016 | tf_op jit(solution)/shard_map/dot_general | solution.py:114
  60.1 1.5 %fusion.22 = (f32[512,512]{1,0:T(8,128)}, f32[512,512]{1,0:T(8,128)}) fusion(f32[512,1024]{1,0:T(8,128)S(1)} %fusion.24), kind=kLoop, calls=%fused_computation.58 | loop fusion | bytes 4194304 | tf_op jit(solution)/shard_map/slice | solution.py:117
  61.6 2.6 %copy.31 = f32[512,512]{0,1:T(8,128)} copy(f32[512,512]{1,0:T(8,128)} %get-tuple-element.245) | data formatting | bytes 2097152 | tf_op jit(solution)/shard_map/slice | solution.py:117
  64.2 2.5 %copy.33 = f32[512,512]{0,1:T(8,128)} copy(f32[512,512]{1,0:T(8,128)} %get-tuple-element.246) | data formatting | bytes 2097152 | tf_op jit(solution)/shard_map/slice | solution.py:118
  66.8 3.4 %bitcast_add_fusion.1 = (f32[512,512]{1,0:T(8,128)}, f32[512,512]{1,0:T(8,128)}) fusion(f32[512,512]{0,1:T(8,128)} %copy.31, f32[512,1024]{1,0:T(8,128)S(1)} %fusion.24, f32[512,512]{0,1:T(8,128)} %copy.33), kind=kLoop, calls=%fused_computation.51 | loop fusion | flops 524288 | bytes 6291456 | tf_op jit(solution)/shard_map/add | solution.py:119
  70.1 1.6 %copy.32 = f32[512,512]{0,1:T(8,128)S(1)} copy(f32[512,512]{1,0:T(8,128)} %get-tuple-element.243) | data formatting | bytes 2097152 | tf_op jit(solution)/shard_map/add | solution.py:119
  72.6 27.1 %all_to_all.10 = f32[8,2,512,64]{2,3,1,0:T(8,128)S(1)} all-to-all(f32[8,2,512,64]{2,3,1,0:T(8,128)S(1)} %copy.35), channel_id=1, replica_groups=mesh['axial'=64,'circ'=8] {'circ'}, dimensions={0} | all-to-all | bytes 4194304 | tf_op jit(solution)/shard_map/all_to_all | solution.py:43
  100.5 32.2 %all_to_all.11 = f32[64,1,1024]{2,1,0:T(1,128)S(1)} all-to-all(f32[64,1,1024]{2,1,0:T(1,128)S(1)} %reshape.428), channel_id=1, replica_groups=mesh['axial'=64,'circ'=8] {'axial'}, dimensions={0} | all-to-all | bytes 524288 | tf_op jit(solution)/shard_map/all_to_all | solution.py:43
  133.1 1.3 reduce
  (47 shorter events, 10.4 us)
Async XLA Ops:
  0.0 9.6 %copy-start.1 = (s32[1,1,3,20]{3,1,2,0:T(1,128)S(1)}, s32[1,1,3,20]{3,1,2,0:T(1,128)}, u32[]{:S(2)}) copy-start(s32[1,1,3,20]{3,1,2,0:T(1,128)} %param.8) | copy-start | bytes 724
  1.4 10.0 %collective-permute-start = (bf16[2,1,128,512]{3,2,1,0:T(8,128)(2,1)S(1)}, bf16[2,1,128,512]{3,2,1,0:T(8,128)(2,1)S(1)}, u32[]{:S(2)}, u32[]{:S(2)}) collective-permute-start(bf16[2,1,128,512]{3,2,1,0:T(8,128)(2,1)S(1)} %get-tuple-element.247), channel_id=1, source_target_pairs={{0,1},{1,2},{2,3},{3,4},{4,5},{5,6},{6,7},{7,0},{8,9},{9,10},{10,1... | collective-permute-start | bytes 786440 | tf_op jit(solution)/shard_map/ppermute | solution.py:21
  5.5 11.7 %collective-permute-start.1 = (bf16[2,1,128,512]{3,2,1,0:T(8,128)(2,1)S(1)}, bf16[2,1,128,512]{3,2,1,0:T(8,128)(2,1)S(1)}, u32[]{:S(2)}, u32[]{:S(2)}) collective-permute-start(bf16[2,1,128,512]{3,2,1,0:T(8,128)(2,1)S(1)} %get-tuple-element.248), channel_id=1, source_target_pairs={{1,0},{2,1},{3,2},{4,3},{5,4},{6,5},{7,6},{0,7},{9,8},{10,9},{11,1... | collective-permute-start | bytes 786440 | tf_op jit(solution)/shard_map/ppermute | solution.py:24
  17.2 13.0 %collective-permute-start.2 = (bf16[1,4,128,512]{3,2,1,0:T(8,128)(2,1)S(1)}, bf16[1,4,128,512]{3,2,1,0:T(8,128)(2,1)S(1)}, u32[]{:S(2)}, u32[]{:S(2)}) collective-permute-start(bf16[1,4,128,512]{3,2,1,0:T(8,128)(2,1)S(1)} %pad_maximum_fusion.1), channel_id=1, source_target_pairs={{8,0},{16,8},{24,16},{32,24},{40,32},{48,40},{56,48},{64,56},{72,6... | collective-permute-start | bytes 1572872 | tf_op jit(solution)/shard_map/ppermute | solution.py:32
  70.1 1.7 %copy-start = (f32[512,512]{1,0:T(8,128)S(1)}, f32[512,512]{1,0:T(8,128)}, u32[]{:S(2)}) copy-start(f32[512,512]{1,0:T(8,128)} %get-tuple-element.244) | copy-start | bytes 3145732
where the time goes:
time: 136 us; the launch traced here: 135 us
  blocking collectives  59.2 us (44%)
  other arithmetic  23.4 us (17%)
  local copies, waits for them, and re-layouts  15.5 us (11%)
  waiting for transfers between devices  13.3 us (10%)
  starting transfers between devices  13 us (10%)
  matrix products  10.5 us (8%)
    all_to_all x2, blocking collectives, sent_and_summed(): lax.all_to_all(blocks, axis, split_axis=0, concat_axis=0, tiled=True)  59.2 us
    dot_general x2, matrix products, slot_products(): jnp.einsum('pcij,pjm->picm', tiles, columns, preferred_element_type=jnp.f...  8.57 us
    another operation x2, other arithmetic  7.03 us
    ppermute x1, waiting for transfers between devices, from_behind(): return lax.ppermute(block, axis, route)  5.83 us
    ppermute x1, waiting for transfers between devices, with_halo(): lax.ppermute(lax.slice_in_dim(block, 0, width, axis=dim), axis, backward)  5.75 us
    reduce_sum x2, other arithmetic, add_row(): jnp.sum(products.reshape(around_blocks, 5, patch_count, 2 * mode_count),...  5.59 us
    ppermute x1, starting transfers between devices, from_behind(): return lax.ppermute(block, axis, route)  4.86 us
    slice x2, local copies, waits for them, and re-layouts, body(): real_part = cross[:, :mode_count]  4.13 us
  transfers between devices with their start and end apart: 3, of which 3 were waited for; matrix products, arithmetic and copies ran while one was open for 2% of the time, Pallas kernels for 0%

commit v1 on v0

v1 whole, which is shorter than its diff:
```python
import numpy as np
import ml_dtypes
import jax
import jax.numpy as jnp
from jax import lax
from jax.sharding import PartitionSpec as P

ALONG = 16
AROUND = 8

axial_decay = 0.125
circ_decay = 0.16
wavenumber = 0.6

OFFSETS = ((0, 0), (0, 1), (1, -1), (1, 0), (1, 1))


def base_tiles():
    patch = np.arange(ALONG * AROUND)
    along_pos = (patch // AROUND).astype(np.float32)
    around_pos = (patch % AROUND).astype(np.float32)
    tiles = []
    for oa, oc in OFFSETS:
        gap_along = np.float32(oa * ALONG) + along_pos[None, :] - along_pos[:, None]
        gap_around = np.float32(oc * AROUND) + around_pos[None, :] - around_pos[:, None]
        envelope = np.exp(
            np.float32(-axial_decay) * np.abs(gap_along) - np.float32(circ_decay) * np.abs(gap_around)
        ).astype(np.float32)
        real_tile = envelope * np.cos(np.float32(wavenumber) * gap_along).astype(np.float32)
        imag_tile = -envelope * np.sin(np.float32(wavenumber) * gap_along).astype(np.float32)
        tiles.append(np.stack([real_tile, imag_tile]))
    return np.stack(tiles).astype(ml_dtypes.bfloat16)


def shifted(block, axes, moves):
    sizes = [lax.axis_size(a) for a in axes]
    total = int(np.prod(sizes))
    pairs = []
    for dst in range(total):
        coords = list(np.unravel_index(dst, sizes))
        ok = True
        for d, (move, cyclic) in enumerate(moves):
            c = coords[d] + move
            if cyclic:
                c %= sizes[d]
            elif not 0 <= c < sizes[d]:
                ok = False
            coords[d] = c
        if ok:
            src = int(np.ravel_multi_index(coords, sizes))
            pairs.append((src, dst))
    return lax.ppermute(block, axes if len(axes) > 1 else axes[0], pairs)


def body(mode_shapes, amplitude, pair_list, pair_counts):
    along_blocks, around_blocks, patch_count, mode_count = mode_shapes.shape
    block_count = along_blocks * around_blocks
    weighted = (mode_shapes * amplitude[..., None]).astype(jnp.bfloat16)

    both = ("axial", "circ")
    right = shifted(weighted[:, 0], ("circ",), ((1, True),))
    left = shifted(weighted[1, 1], ("circ",), ((-1, True),))
    ahead = shifted(weighted[0], ("axial",), ((1, False),))
    ahead_left = shifted(weighted[0, 1], both, ((1, False), (-1, True)))
    ahead_right = shifted(weighted[0, 0], both, ((1, False), (1, True)))

    def window(x, y):
        if x < 2 and 0 <= y < 2:
            return weighted[x, y]
        if x < 2 and y == 2:
            return right[x]
        if x == 1 and y == -1:
            return left
        if x == 2 and 0 <= y < 2:
            return ahead[y]
        if x == 2 and y == -1:
            return ahead_left
        return ahead_right

    columns = jnp.stack(
        [
            jnp.concatenate([window(i + oa, j + oc) for oa, oc in OFFSETS], axis=0)
            for i in range(along_blocks)
            for j in range(around_blocks)
        ]
    )

    listing = pair_list[0, 0]
    slot_total = listing.shape[1]
    slot = jnp.arange(slot_total, dtype=jnp.int32)
    valid = (slot < pair_counts[0, 0]).astype(jnp.float32)
    half = jnp.where((listing[1] == 0) & (listing[2] == 0), 0.5, 1.0).astype(jnp.float32)
    kind = listing[1] * 3 + listing[2]
    row_hot = (listing[0][None, :] == jnp.arange(block_count)[:, None]).astype(jnp.float32)
    kind_hot = (kind[None, :] == jnp.arange(len(OFFSETS))[:, None]).astype(jnp.float32)
    weight = jnp.einsum("rs,ks,s->rk", row_hot, kind_hot, valid * half)

    tiles = jnp.asarray(base_tiles())
    lhs = (tiles.astype(jnp.float32)[None] * weight[:, :, None, None, None]).astype(jnp.bfloat16)
    lhs = jnp.transpose(lhs, (0, 2, 3, 1, 4)).reshape(block_count, 2 * patch_count, -1)
    row_sums = lax.dot_general(
        lhs, columns, (((2,), (1,)), ((0,), (0,))), preferred_element_type=jnp.float32
    )
    rounded = row_sums.astype(jnp.bfloat16).reshape(block_count, 2, patch_count, mode_count)
    rounded = jnp.transpose(rounded, (1, 0, 2, 3)).reshape(2, block_count * patch_count, mode_count)
    local = weighted.reshape(block_count * patch_count, mode_count)
    first = jnp.stack([jnp.concatenate([local, rounded[q]], axis=0) for q in range(2)])
    second = jnp.stack(
        [jnp.concatenate([rounded[0], local], axis=0), jnp.concatenate([rounded[1], -local], axis=0)]
    )
    summand = lax.dot_general(
        first, second, (((1,), (1,)), ((0,), (0,))), preferred_element_type=jnp.float32
    )
    n_ax = lax.axis_size("axial")
    n_ci = lax.axis_size("circ")
    rows = mode_count // n_ax
    cols = mode_count // n_ci
    arranged = summand.reshape(2, n_ax, rows, n_ci, cols).transpose(1, 3, 0, 2, 4)
    arranged = arranged.reshape(n_ax * n_ci, 2, rows, cols)
    result = lax.psum_scatter(arranged, both, scatter_dimension=0, tiled=True)
    return result.reshape(2, rows, cols)


def solution(mesh):
    in_specs = (
        P("axial", "circ", None, None),
        P("axial", "circ", None),
        P("axial", "circ", None, None),
        P("axial", "circ"),
    )
    out_specs = P(None, "axial", "circ")
    return jax.shard_map(body, mesh=mesh, in_specs=in_specs, out_specs=out_specs, check_vma=False)
```

time: 136 us -> 2620 us (19.26)
  waiting for transfers between devices: 13.3 us -> 2560 us
  blocking collectives: 59.2 us -> 0 us
    reduce_scatter x0 -> x1, waiting for transfers between devices: none -> 2560 us  [body(): result = lax.psum_scatter(arranged, both, scatter_dimension=0, tiled=True)]
    all_to_all x2 -> x0, blocking collectives: 59.2 us -> none  [sent_and_summed(): lax.all_to_all(blocks, axis, split_axis=0, concat_axis=0, tiled=True)]
  transfers between devices with their start and end apart: 3 -> 6, of which waited for: 3 -> 3; matrix products, arithmetic and copies ran while one was open for 2% -> 0% of each run, Pallas kernels for 0% -> 0%
where the time goes in v1:
time: 2620 us; the launch traced here: 2610 us
  waiting for transfers between devices  2560 us (98%)
    reduce_scatter x1, waiting for transfers between devices, body(): result = lax.psum_scatter(arranged, both, scatter_dimension=0, tiled=True)  2560 us
  transfers between devices with their start and end apart: 6, of which 3 were waited for; matrix products, arithmetic and copies ran while one was open for 0% of the time, Pallas kernels for 0%

profile of v1, /device:TPU:1, one launch (start us, length us, event | category | flops | bytes accessed | tf_op | source)
XLA Modules:
  0.0 2608.5 jit_solution(16779051587262759610)
XLA Ops:
  6.5 0.0 reduce-scatter.2.cloned.1.call-start
  6.5 1.4 multiply_convert_fusion.2
  7.9 6.2 collective-permute-start.1
  14.2 4.5 collective-permute-start.3
  18.7 3.6 collective-permute-start
  22.3 1.9 collective-permute-start.2
  24.3 2.7 collective-permute-start.4
  26.9 0.1 bitcast_negate_fusion
  27.0 0.0 copy-start.1
  27.8 0.1 fusion.32
  27.9 0.1 broadcast_bitcast_fusion
  28.0 0.0 collective-permute-done
  28.1 0.0 collective-permute-done.1
  28.2 3.5 collective-permute-done.2
  31.7 0.0 collective-permute-done.3
  31.8 0.8 collective-permute-done.4
  32.6 1.0 fusion.15
  33.6 0.1 fusion.41
  33.7 0.4 maximum_bitcast_fusion
  34.1 1.3 fusion.8
  35.4 2.4 reshape.56
  37.8 5.1 copy.9
  42.9 0.0 reduce-scatter.2.cloned.1.call-update
  43.0 2558.7 %reduce-scatter.2.cloned.1.call-done = f32[1,2,8,64]{3,2,1,0:T(8,128)} async-done(((f32[512,2,8,64]{3,2,1,0:T(8,128)}), f32[1,2,8,64]{3,2,1,0:T(8,128)}) %reduce-scatter.2.cloned.1.call-update) | async-done | bytes 4112 | tf_op jit(solution)/shard_map/reduce_scatter | solution.py:120
  (21 shorter events, 0.3 us)
Async XLA Ops:
  6.5 21.2 copy-start
  6.5 2595.1 %reduce-scatter.2.cloned.1.call-start = ((), (), s32[]{:S(2)}) async-start(), calls=%async_computation.1 | async-start | bytes 4202496 | tf_op jit(solution)/shard_map/reduce_scatter | solution.py:120
  7.9 20.1 collective-permute-start.1
  14.2 17.5 collective-permute-start.3
  18.7 9.3 collective-permute-start
  22.3 9.3 collective-permute-start.2
  24.3 8.3 collective-permute-start.4
  27.0 5.5 copy-start.1
Sparse Core Ops, SparseCore 0:
  43.1 2558.5 reduce-scatter.1

commit v2 on v1

--- a/solution.py
+++ b/solution.py
@@ -113,12 +113,16 @@
     )
     n_ax = lax.axis_size("axial")
     n_ci = lax.axis_size("circ")
+    cols = mode_count // n_ci
     rows = mode_count // n_ax
-    cols = mode_count // n_ci
-    arranged = summand.reshape(2, n_ax, rows, n_ci, cols).transpose(1, 3, 0, 2, 4)
-    arranged = arranged.reshape(n_ax * n_ci, 2, rows, cols)
-    result = lax.psum_scatter(arranged, both, scatter_dimension=0, tiled=True)
-    return result.reshape(2, rows, cols)
+    parts = lax.all_to_all(
+        summand.reshape(2, mode_count, n_ci, cols), "circ", 2, 0, tiled=True
+    )
+    partial_value = parts.reshape(n_ci, 2, mode_count, cols).sum(axis=0)
+    parts = lax.all_to_all(
+        partial_value.reshape(2, n_ax, rows, cols), "axial", 1, 0, tiled=True
+    )
+    return parts.reshape(n_ax, 2, rows, cols).sum(axis=0)
 
 
 def solution(mesh):

time: 2620 us -> 96 us (0.04)
  waiting for transfers between devices: 2560 us -> 0.56 us
  blocking collectives: 0 us -> 60.7 us
    reduce_scatter x1 -> x0, waiting for transfers between devices: 2560 us -> none  [body(): result = lax.psum_scatter(arranged, both, scatter_dimension=0, tiled=True)]
    all_to_all x0 -> x2, blocking collectives: none -> 60.7 us  [the longest x1 35.3 us: body(): lax.all_to_all(summand.reshape(2, mode_count, n_ci, cols), 'circ', 2, 0,...]
  transfers between devices with their start and end apart: 6 -> 5, of which waited for: 3 -> 1; matrix products, arithmetic and copies ran while one was open for 0% -> 4% of each run, Pallas kernels for 0% -> 0%
where the time goes in v2:
time: 96 us; the launch traced here: 95.5 us
  blocking collectives  60.7 us (63%)
  starting transfers between devices  19.9 us (21%)
  local copies, waits for them, and re-layouts  5.76 us (6%)
  other arithmetic  4.17 us (4%)
  matrix products  3.51 us (4%)
    all_to_all x1, blocking collectives, body(): lax.all_to_all(summand.reshape(2, mode_count, n_ci, cols), 'circ', 2, 0,...  35.3 us
    all_to_all x1, blocking collectives, body(): lax.all_to_all(partial_value.reshape(2, n_ax, rows, cols), 'axial', 1, 0,...  25.3 us
    ppermute x5, starting transfers between devices, shifted(): return lax.ppermute(block, axes if len(axes) > 1 else axes[0], pairs)  19.9 us
    unnamed x17, local copies, waits for them, and re-layouts  3.31 us
    dot_general x1, matrix products, body(): lax.dot_general(lhs, columns, (((2,), (1,)), ((0,), (0,))), preferred_ele...  2.1 us
  transfers between devices with their start and end apart: 5, of which 1 were waited for; matrix products, arithmetic and copies ran while one was open for 4% of the time, Pallas kernels for 0%

profile of v2, /device:TPU:1, one launch (start us, length us, event | category | flops | bytes accessed | tf_op | source)
XLA Modules:
  0.0 95.5 jit_solution(9433646576498780937)
XLA Ops:
  0.0 1.4 %multiply_convert_fusion.2 = bf16[2,2,128,512]{3,2,1,0:T(8,128)(2,1)S(1)} fusion(f32[2,2,128,512]{3,2,1,0:T(8,128)} %param.5, f32[2,2,128]{2,1,0:T(2,128)} %param.6), kind=kLoop, calls=%fused_computation.25 | loop fusion | flops 524288 | bytes 1574912 | tf_op jit(solution)/shard_map/convert_element_type | solution.py:58
  1.4 4.0 %collective-permute-start = (bf16[128,512]{1,0:T(8,128)(2,1)S(1)}, bf16[128,512]{1,0:T(8,128)(2,1)S(1)}, u32[]{:S(2)}, u32[]{:S(2)}) collective-permute-start(bf16[128,512]{1,0:T(8,128)(2,1)S(1)} %get-tuple-element.18), channel_id=1, source_target_pairs={{7,0},{0,1},{1,2},{2,3},{3,4},{4,5},{5,6},{6,7},{15,8},{8,9},{9,10... | collective-permute-start | bytes 393224 | tf_op jit(solution)/shard_map/ppermute | solution.py:52
  5.5 4.1 %collective-permute-start.1 = (bf16[2,128,512]{2,1,0:T(8,128)(2,1)S(1)}, bf16[2,128,512]{2,1,0:T(8,128)(2,1)S(1)}, u32[]{:S(2)}, u32[]{:S(2)}) collective-permute-start(bf16[2,128,512]{2,1,0:T(8,128)(2,1)S(1)} %slice_bitcast_fusion.1), channel_id=1, source_target_pairs={{1,0},{2,1},{3,2},{4,3},{5,4},{6,5},{7,6},{0,7},{9,8},{10,9},{11,1... | collective-permute-start | bytes 786440 | tf_op jit(solution)/shard_map/ppermute | solution.py:52
  9.6 6.1 %collective-permute-start.2 = (bf16[128,512]{1,0:T(8,128)(2,1)S(1)}, bf16[128,512]{1,0:T(8,128)(2,1)S(1)}, u32[]{:S(2)}, u32[]{:S(2)}) collective-permute-start(bf16[128,512]{1,0:T(8,128)(2,1)S(1)} %get-tuple-element.19), channel_id=1, source_target_pairs={{15,0},{8,1},{9,2},{10,3},{11,4},{12,5},{13,6},{14,7},{23,8},{16,9... | collective-permute-start | bytes 393224 | tf_op jit(solution)/shard_map/ppermute | solution.py:52
  15.7 3.8 %collective-permute-start.3 = (bf16[2,128,512]{2,1,0:T(8,128)(2,1)S(1)}, bf16[2,128,512]{2,1,0:T(8,128)(2,1)S(1)}, u32[]{:S(2)}, u32[]{:S(2)}) collective-permute-start(bf16[2,128,512]{2,1,0:T(8,128)(2,1)S(1)} %slice_bitcast_fusion), channel_id=1, source_target_pairs={{8,0},{16,8},{24,16},{32,24},{40,32},{48,40},{56,48},{64,56},{72,6... | collective-permute-start | bytes 786440 | tf_op jit(solution)/shard_map/ppermute | solution.py:52
  19.5 1.9 %collective-permute-start.4 = (bf16[128,512]{1,0:T(8,128)(2,1)S(1)}, bf16[128,512]{1,0:T(8,128)(2,1)S(1)}, u32[]{:S(2)}, u32[]{:S(2)}) collective-permute-start(bf16[128,512]{1,0:T(8,128)(2,1)S(1)} %get-tuple-element.20), channel_id=1, source_target_pairs={{9,0},{10,1},{11,2},{12,3},{13,4},{14,5},{15,6},{8,7},{17,8},{18,9... | collective-permute-start | bytes 393224 | tf_op jit(solution)/shard_map/ppermute | solution.py:52
  21.4 0.7 constant_dynamic-update-slice_fusion.3
  23.3 0.7 constant_dynamic-update-slice_fusion.2
  24.0 0.7 constant_dynamic-update-slice_fusion.1
  24.6 0.7 fusion.31
  25.3 0.7 constant_dynamic-update-slice_fusion
  26.1 0.6 collective-permute-done.4
  26.7 2.1 %fusion.15 = bf16[4,256,512]{2,1,0:T(8,128)(2,1)S(1)} fusion(bf16[1,640,512]{2,1,0:T(8,128)(2,1)S(1)} %bitcast.98, bf16[1,640,512]{2,1,0:T(8,128)(2,1)S(1)} %bitcast.99, bf16[1,640,512]{2,1,0:T(8,128)(2,1)S(1)} %bitcast.100, bf16[1,640,512]{2,1,0:T(8,128)(2,1)} %bitcast.101, f32[4,640]{1,0:T(4,128)S(1)} %bitcast.102, f32[256,640]{1,0:T(8,128)S(1)} %copy-done.1), kind=kOutput, calls=%fused_computation.16 | convolution fusion | flops 676855808 | bytes 4335616 | tf_op jit(solution)/shard_map/dot_general | solution.py:101
  28.9 0.2 copy.42
  29.1 0.2 copy.43
  29.4 0.5 maximum_bitcast_fusion
  29.9 1.3 %fusion.8 = f32[2,512,512]{1,2,0:T(8,128)S(1)} fusion(bf16[1,1024,512]{1,2,0:T(8,128)(2,1)S(1)} %get-tuple-element.9, bf16[1,1024,512]{1,2,0:T(8,128)(2,1)S(1)} %get-tuple-element.6, bf16[1,1024,512]{1,2,0:T(8,128)(2,1)S(1)} %get-tuple-element.10, bf16[1,1024,512]{1,2,0:T(8,128)(2,1)S(1)} %get-tuple-element.5), kind=kOutput, calls=%fused_computation.9 | convolution fusion | flops 1075838976 | bytes 6291456 | tf_op jit(solution)/shard_map/dot_general | solution.py:111
  31.4 35.3 %all_to_all.8 = f32[2,512,8,64]{1,3,0,2:T(8,128)S(1)} all-to-all(f32[2,512,8,64]{1,3,0,2:T(8,128)S(1)} %copy.37), channel_id=1, replica_groups=mesh['axial'=64,'circ'=8] {'circ'}, dimensions={2} | all-to-all | bytes 4194304 | tf_op jit(solution)/shard_map/all_to_all | solution.py:118
  66.8 0.2 reduce_sum.18
  67.2 0.3 reshape.59
  67.6 25.3 %all_to_all.9 = f32[64,1,1024]{2,1,0:T(1,128)S(1)} all-to-all(f32[64,1,1024]{2,1,0:T(1,128)S(1)} %reshape.59), channel_id=1, replica_groups=mesh['axial'=64,'circ'=8] {'axial'}, dimensions={0} | all-to-all | bytes 524288 | tf_op jit(solution)/shard_map/all_to_all | solution.py:122
  92.9 0.5 broadcast.48
  93.4 1.3 %reduce.6 = f32[64,1024]{1,0:T(8,128)S(1)} reduce(f32[64,1,1024]{2,1,0:T(1,128)S(1)} %all_to_all.9, f32[]{:T(128)} %broadcast.48), dimensions={1}, to_apply=%all_to_all.5.reduce_sub_computation | reduce | bytes 524292 | tf_op jit(solution)/shard_map/all_to_all | solution.py:122
  94.8 0.7 bitcast_reduce_fusion
  (30 shorter events, 1.4 us)
Async XLA Ops:
  0.0 22.1 %copy-start = (s32[1,1,3,20]{3,1,2,0:T(1,128)S(1)}, s32[1,1,3,20]{3,1,2,0:T(1,128)}, u32[]{:S(2)}) copy-start(s32[1,1,3,20]{3,1,2,0:T(1,128)} %param.7) | copy-start | bytes 724
  1.4 22.5 %collective-permute-start = (bf16[128,512]{1,0:T(8,128)(2,1)S(1)}, bf16[128,512]{1,0:T(8,128)(2,1)S(1)}, u32[]{:S(2)}, u32[]{:S(2)}) collective-permute-start(bf16[128,512]{1,0:T(8,128)(2,1)S(1)} %get-tuple-element.18), channel_id=1, source_target_pairs={{7,0},{0,1},{1,2},{2,3},{3,4},{4,5},{5,6},{6,7},{15,8},{8,9},{9,10... | collective-permute-start | bytes 393224 | tf_op jit(solution)/shard_map/ppermute | solution.py:52
  5.5 19.8 %collective-permute-start.1 = (bf16[2,128,512]{2,1,0:T(8,128)(2,1)S(1)}, bf16[2,128,512]{2,1,0:T(8,128)(2,1)S(1)}, u32[]{:S(2)}, u32[]{:S(2)}) collective-permute-start(bf16[2,128,512]{2,1,0:T(8,128)(2,1)S(1)} %slice_bitcast_fusion.1), channel_id=1, source_target_pairs={{1,0},{2,1},{3,2},{4,3},{5,4},{6,5},{7,6},{0,7},{9,8},{10,9},{11,1... | collective-permute-start | bytes 786440 | tf_op jit(solution)/shard_map/ppermute | solution.py:52
  9.6 16.4 %collective-permute-start.2 = (bf16[128,512]{1,0:T(8,128)(2,1)S(1)}, bf16[128,512]{1,0:T(8,128)(2,1)S(1)}, u32[]{:S(2)}, u32[]{:S(2)}) collective-permute-start(bf16[128,512]{1,0:T(8,128)(2,1)S(1)} %get-tuple-element.19), channel_id=1, source_target_pairs={{15,0},{8,1},{9,2},{10,3},{11,4},{12,5},{13,6},{14,7},{23,8},{16,9... | collective-permute-start | bytes 393224 | tf_op jit(solution)/shard_map/ppermute | solution.py:52
  15.7 10.4 %collective-permute-start.3 = (bf16[2,128,512]{2,1,0:T(8,128)(2,1)S(1)}, bf16[2,128,512]{2,1,0:T(8,128)(2,1)S(1)}, u32[]{:S(2)}, u32[]{:S(2)}) collective-permute-start(bf16[2,128,512]{2,1,0:T(8,128)(2,1)S(1)} %slice_bitcast_fusion), channel_id=1, source_target_pairs={{8,0},{16,8},{24,16},{32,24},{40,32},{48,40},{56,48},{64,56},{72,6... | collective-permute-start | bytes 786440 | tf_op jit(solution)/shard_map/ppermute | solution.py:52
  19.5 7.2 %collective-permute-start.4 = (bf16[128,512]{1,0:T(8,128)(2,1)S(1)}, bf16[128,512]{1,0:T(8,128)(2,1)S(1)}, u32[]{:S(2)}, u32[]{:S(2)}) collective-permute-start(bf16[128,512]{1,0:T(8,128)(2,1)S(1)} %get-tuple-element.20), channel_id=1, source_target_pairs={{9,0},{10,1},{11,2},{12,3},{13,4},{14,5},{15,6},{8,7},{17,8},{18,9... | collective-permute-start | bytes 393224 | tf_op jit(solution)/shard_map/ppermute | solution.py:52
  23.3 3.4 %copy-start.1 = (f32[256,640]{1,0:T(8,128)S(1)}, f32[256,640]{1,0:T(8,128)}, u32[]{:S(2)}) copy-start(f32[256,640]{1,0:T(8,128)} %constant.21) | copy-start | bytes 1966084

commit v3 on v1

--- a/solution.py
+++ b/solution.py
@@ -3,7 +3,7 @@
 import jax
 import jax.numpy as jnp
 from jax import lax
-from jax.sharding import PartitionSpec as P
+from jax.sharding import Mesh, PartitionSpec as P
 
 ALONG = 16
 AROUND = 8
@@ -32,8 +32,16 @@
     return np.stack(tiles).astype(ml_dtypes.bfloat16)
 
 
+AXIAL = ("y_hi", "z", "core")
+CIRC = ("x", "y_lo")
+
+
+def group_size(axes):
+    return int(np.prod([lax.axis_size(a) for a in axes]))
+
+
 def shifted(block, axes, moves):
-    sizes = [lax.axis_size(a) for a in axes]
+    sizes = [group_size(a) for a in axes]
     total = int(np.prod(sizes))
     pairs = []
     for dst in range(total):
@@ -49,7 +57,7 @@
         if ok:
             src = int(np.ravel_multi_index(coords, sizes))
             pairs.append((src, dst))
-    return lax.ppermute(block, axes if len(axes) > 1 else axes[0], pairs)
+    return lax.ppermute(block, sum(axes, ()), pairs)
 
 
 def body(mode_shapes, amplitude, pair_list, pair_counts):
@@ -57,10 +65,10 @@
     block_count = along_blocks * around_blocks
     weighted = (mode_shapes * amplitude[..., None]).astype(jnp.bfloat16)
 
-    both = ("axial", "circ")
-    right = shifted(weighted[:, 0], ("circ",), ((1, True),))
-    left = shifted(weighted[1, 1], ("circ",), ((-1, True),))
-    ahead = shifted(weighted[0], ("axial",), ((1, False),))
+    both = (AXIAL, CIRC)
+    right = shifted(weighted[:, 0], (CIRC,), ((1, True),))
+    left = shifted(weighted[1, 1], (CIRC,), ((-1, True),))
+    ahead = shifted(weighted[0], (AXIAL,), ((1, False),))
     ahead_left = shifted(weighted[0, 1], both, ((1, False), (-1, True)))
     ahead_right = shifted(weighted[0, 0], both, ((1, False), (1, True)))
 
@@ -111,22 +119,27 @@
     summand = lax.dot_general(
         first, second, (((1,), (1,)), ((0,), (0,))), preferred_element_type=jnp.float32
     )
-    n_ax = lax.axis_size("axial")
-    n_ci = lax.axis_size("circ")
-    rows = mode_count // n_ax
+    n_core = lax.axis_size("core")
+    outer = group_size(AXIAL) // n_core
+    n_ci = group_size(CIRC)
     cols = mode_count // n_ci
-    arranged = summand.reshape(2, n_ax, rows, n_ci, cols).transpose(1, 3, 0, 2, 4)
-    arranged = arranged.reshape(n_ax * n_ci, 2, rows, cols)
-    result = lax.psum_scatter(arranged, both, scatter_dimension=0, tiled=True)
-    return result.reshape(2, rows, cols)
+    rows = mode_count // (outer * n_core)
+    arranged = summand.reshape(2, outer, n_core, rows, n_ci, cols).transpose(4, 2, 1, 0, 3, 5)
+    arranged = arranged.reshape(n_ci * n_core, outer * 2 * rows * cols)
+    parts = lax.all_to_all(arranged, CIRC + ("core",), 0, 0, tiled=True)
+    partial_value = parts.reshape(n_ci * n_core, outer, 2 * rows * cols).sum(axis=0)
+    parts = lax.all_to_all(partial_value, AXIAL[:-1], 0, 0, tiled=True)
+    return parts.sum(axis=0).reshape(2, rows, cols)
 
 
 def solution(mesh):
+    sizes = [mesh.shape["axial"] // 16, 8, 2, mesh.shape["circ"] // 2, 2]
+    fine = Mesh(mesh.devices.reshape(sizes), AXIAL + CIRC)
     in_specs = (
-        P("axial", "circ", None, None),
-        P("axial", "circ", None),
-        P("axial", "circ", None, None),
-        P("axial", "circ"),
+        P(AXIAL, CIRC, None, None),
+        P(AXIAL, CIRC, None),
+        P(AXIAL, CIRC, None, None),
+        P(AXIAL, CIRC),
     )
-    out_specs = P(None, "axial", "circ")
-    return jax.shard_map(body, mesh=mesh, in_specs=in_specs, out_specs=out_specs, check_vma=False)
+    out_specs = P(None, AXIAL, CIRC)
+    return jax.shard_map(body, mesh=fine, in_specs=in_specs, out_specs=out_specs, check_vma=False)

time: 2620 us -> 105 us (0.04)
  waiting for transfers between devices: 2560 us -> 4.28 us
  blocking collectives: 0 us -> 59.8 us
    reduce_scatter x1 -> x0, waiting for transfers between devices: 2560 us -> none  [body(): result = lax.psum_scatter(arranged, both, scatter_dimension=0, tiled=True)]
    all_to_all x0 -> x2, blocking collectives: none -> 59.8 us  [the longest x1 33.5 us: body(): parts = lax.all_to_all(arranged, CIRC + ('core',), 0, 0, tiled=True)]
  transfers between devices with their start and end apart: 6 -> 5, of which waited for: 3 -> 2; matrix products, arithmetic and copies ran while one was open for 0% -> 0% of each run, Pallas kernels for 0% -> 0%
where the time goes in v3:
time: 105 us; the launch traced here: 104 us
  blocking collectives  59.8 us (57%)
  starting transfers between devices  18.9 us (18%)
  local copies, waits for them, and re-layouts  13 us (12%)
  other arithmetic  4.94 us (5%)
  waiting for transfers between devices  4.28 us (4%)
  matrix products  2.45 us (2%)
    all_to_all x1, blocking collectives, body(): parts = lax.all_to_all(arranged, CIRC + ('core',), 0, 0, tiled=True)  33.5 us
    all_to_all x1, blocking collectives, body(): parts = lax.all_to_all(partial_value, AXIAL[:-1], 0, 0, tiled=True)  26.3 us
    ppermute x5, starting transfers between devices, shifted(): return lax.ppermute(block, sum(axes, ()), pairs)  18.9 us
    reshape x2, local copies, waits for them, and re-layouts, body(): summand.reshape(2, outer, n_core, rows, n_ci, cols)  7.36 us
    all_to_all x1, local copies, waits for them, and re-layouts, body(): parts = lax.all_to_all(arranged, CIRC + ('core',), 0, 0, tiled=True)  4.52 us
    ppermute x5, waiting for transfers between devices, shifted(): return lax.ppermute(block, sum(axes, ()), pairs)  4.28 us
    reduce_sum x1, other arithmetic, body(): parts.reshape(n_ci * n_core, outer, 2 * rows * cols).sum(axis=0)  2.95 us
  transfers between devices with their start and end apart: 5, of which 2 were waited for; matrix products, arithmetic and copies ran while one was open for 0% of the time, Pallas kernels for 0%

profile of v3, /device:TPU:1, one launch (start us, length us, event | category | flops | bytes accessed | tf_op | source)
XLA Modules:
  0.0 104.3 jit_solution(5970471237688473992)
XLA Ops:
  0.0 1.4 %multiply_convert_fusion.2 = bf16[2,2,128,512]{3,2,1,0:T(8,128)(2,1)S(1)} fusion(f32[2,2,128,512]{3,2,1,0:T(8,128)} %param.5, f32[2,2,128]{2,1,0:T(2,128)} %param.6), kind=kLoop, calls=%fused_computation.26 | loop fusion | flops 524288 | bytes 1574912 | tf_op jit(solution)/shard_map/convert_element_type | solution.py:66
  1.4 6.2 %collective-permute-start.1 = (bf16[2,128,512]{2,1,0:T(8,128)(2,1)S(1)}, bf16[2,128,512]{2,1,0:T(8,128)(2,1)S(1)}, u32[]{:S(2)}, u32[]{:S(2)}) collective-permute-start(bf16[2,128,512]{2,1,0:T(8,128)(2,1)S(1)} %slice_bitcast_fusion.1), channel_id=1, source_target_pairs={{1,0},{2,1},{3,2},{4,3},{5,4},{6,5},{7,6},{0,7},{9,8},{10,9},{11,1... | collective-permute-start | bytes 786440 | tf_op jit(solution)/shard_map/ppermute | solution.py:60
  7.7 4.5 %collective-permute-start.3 = (bf16[2,128,512]{2,1,0:T(8,128)(2,1)S(1)}, bf16[2,128,512]{2,1,0:T(8,128)(2,1)S(1)}, u32[]{:S(2)}, u32[]{:S(2)}) collective-permute-start(bf16[2,128,512]{2,1,0:T(8,128)(2,1)S(1)} %slice_bitcast_fusion), channel_id=1, source_target_pairs={{8,0},{16,8},{24,16},{32,24},{40,32},{48,40},{56,48},{64,56},{72,6... | collective-permute-start | bytes 786440 | tf_op jit(solution)/shard_map/ppermute | solution.py:60
  12.2 3.6 %collective-permute-start = (bf16[128,512]{1,0:T(8,128)(2,1)S(1)}, bf16[128,512]{1,0:T(8,128)(2,1)S(1)}, u32[]{:S(2)}, u32[]{:S(2)}) collective-permute-start(bf16[128,512]{1,0:T(8,128)(2,1)S(1)} %get-tuple-element.18), channel_id=1, source_target_pairs={{7,0},{0,1},{1,2},{2,3},{3,4},{4,5},{5,6},{6,7},{15,8},{8,9},{9,10... | collective-permute-start | bytes 393224 | tf_op jit(solution)/shard_map/ppermute | solution.py:60
  15.8 1.9 %collective-permute-start.2 = (bf16[128,512]{1,0:T(8,128)(2,1)S(1)}, bf16[128,512]{1,0:T(8,128)(2,1)S(1)}, u32[]{:S(2)}, u32[]{:S(2)}) collective-permute-start(bf16[128,512]{1,0:T(8,128)(2,1)S(1)} %get-tuple-element.19), channel_id=1, source_target_pairs={{15,0},{8,1},{9,2},{10,3},{11,4},{12,5},{13,6},{14,7},{23,8},{16,9... | collective-permute-start | bytes 393224 | tf_op jit(solution)/shard_map/ppermute | solution.py:60
  17.7 2.7 %collective-permute-start.4 = (bf16[128,512]{1,0:T(8,128)(2,1)S(1)}, bf16[128,512]{1,0:T(8,128)(2,1)S(1)}, u32[]{:S(2)}, u32[]{:S(2)}) collective-permute-start(bf16[128,512]{1,0:T(8,128)(2,1)S(1)} %get-tuple-element.20), channel_id=1, source_target_pairs={{9,0},{10,1},{11,2},{12,3},{13,4},{14,5},{15,6},{8,7},{17,8},{18,9... | collective-permute-start | bytes 393224 | tf_op jit(solution)/shard_map/ppermute | solution.py:60
  20.4 0.1 bitcast_negate_fusion
  20.5 0.0 copy-start.1
  21.3 0.1 fusion.32
  21.4 0.1 broadcast_bitcast_fusion
  21.6 3.5 %collective-permute-done.2 = bf16[128,512]{1,0:T(8,128)(2,1)S(1)} collective-permute-done((bf16[128,512]{1,0:T(8,128)(2,1)S(1)}, bf16[128,512]{1,0:T(8,128)(2,1)S(1)}, u32[]{:S(2)}, u32[]{:S(2)}) %collective-permute-start.2) | collective-permute-done | bytes 131104 | tf_op jit(solution)/shard_map/ppermute | solution.py:60
  25.3 0.8 collective-permute-done.4
  26.1 1.0 fusion.15
  27.1 0.1 fusion.41
  27.2 0.4 maximum_bitcast_fusion
  27.6 1.3 %fusion.8 = f32[2,512,512]{2,1,0:T(8,128)S(1)} fusion(bf16[1,1024,512]{2,1,0:T(8,128)(2,1)S(1)} %get-tuple-element.9, bf16[1,1024,512]{2,1,0:T(8,128)(2,1)S(1)} %get-tuple-element.6, bf16[1,1024,512]{2,1,0:T(8,128)(2,1)S(1)} %get-tuple-element.10, bf16[1,1024,512]{2,1,0:T(8,128)(2,1)S(1)} %get-tuple-element.5), kind=kOutput, calls=%fused_computation.10 | convolution fusion | flops 1075838976 | bytes 6291456 | tf_op jit(solution)/shard_map/dot_general | solution.py:119
  28.9 2.4 %reshape.62 = f32[2,32,2,8,8,64]{5,4,3,2,1,0:T(8,128)} reshape(f32[2,512,512]{2,1,0:T(8,128)S(1)} %fusion.8) | data formatting | bytes 4194304 | tf_op jit(solution)/shard_map/reshape | solution.py:127
  31.3 5.0 %copy.24 = f32[2,32,2,8,8,64]{5,3,0,1,2,4:T(8,128)} copy(f32[2,32,2,8,8,64]{5,4,3,2,1,0:T(8,128)} %reshape.62) | data formatting | bytes 4194304 | tf_op jit(solution)/shard_map/reshape | solution.py:127
  36.3 4.5 %all_to_all.16 = f32[16,1,32768]{2,1,0:T(1,128)S(1)} reshape(f32[8,2,32,2,8,64]{5,4,3,2,1,0:T(8,128)} %bitcast.93) | data formatting | bytes 4194304 | tf_op jit(solution)/shard_map/all_to_all | solution.py:129
  40.8 33.5 %all_to_all.19 = f32[16,1,32768]{2,1,0:T(1,128)} all-to-all(f32[16,1,32768]{2,1,0:T(1,128)S(1)} %all_to_all.16), channel_id=1, replica_groups=mesh['y_hi'=4,'z'=8,'core'=2,'x'=4,'y_lo'=2] {'x','y_lo','core'}, dimensions={0} | all-to-all | bytes 4194304 | tf_op jit(solution)/shard_map/all_to_all | solution.py:129
  74.3 3.0 %reduce_sum.18 = f32[32768]{0:T(1024)S(1)} reduce(f32[16,1,32768]{2,1,0:T(1,128)} %all_to_all.19, f32[]{:T(128)} %constant.13.clone.1), dimensions={0,1}, to_apply=%region_0.1 | reduce | flops 491520 | bytes 2228228 | tf_op jit(solution)/shard_map/reduce_sum | solution.py:130
  77.2 26.3 %all_to_all.20 = f32[32,1,1024]{2,1,0:T(1,128)S(1)} all-to-all(f32[32,1,1024]{2,1,0:T(1,128)S(1)} %bitcast.97), channel_id=1, replica_groups=mesh['y_hi'=4,'z'=8,'core'=2,'x'=4,'y_lo'=2] {'y_hi','z'}, dimensions={0} | all-to-all | bytes 262144 | tf_op jit(solution)/shard_map/all_to_all | solution.py:131
  103.5 0.1 reduce_sum.19
  103.6 0.7 reshape.63
  (24 shorter events, 0.3 us)
Async XLA Ops:
  0.0 21.2 %copy-start = (s32[1,1,3,20]{3,1,2,0:T(1,128)S(1)}, s32[1,1,3,20]{3,1,2,0:T(1,128)}, u32[]{:S(2)}) copy-start(s32[1,1,3,20]{3,1,2,0:T(1,128)} %param.7) | copy-start | bytes 724
  1.4 20.1 %collective-permute-start.1 = (bf16[2,128,512]{2,1,0:T(8,128)(2,1)S(1)}, bf16[2,128,512]{2,1,0:T(8,128)(2,1)S(1)}, u32[]{:S(2)}, u32[]{:S(2)}) collective-permute-start(bf16[2,128,512]{2,1,0:T(8,128)(2,1)S(1)} %slice_bitcast_fusion.1), channel_id=1, source_target_pairs={{1,0},{2,1},{3,2},{4,3},{5,4},{6,5},{7,6},{0,7},{9,8},{10,9},{11,1... | collective-permute-start | bytes 786440 | tf_op jit(solution)/shard_map/ppermute | solution.py:60
  7.7 17.5 %collective-permute-start.3 = (bf16[2,128,512]{2,1,0:T(8,128)(2,1)S(1)}, bf16[2,128,512]{2,1,0:T(8,128)(2,1)S(1)}, u32[]{:S(2)}, u32[]{:S(2)}) collective-permute-start(bf16[2,128,512]{2,1,0:T(8,128)(2,1)S(1)} %slice_bitcast_fusion), channel_id=1, source_target_pairs={{8,0},{16,8},{24,16},{32,24},{40,32},{48,40},{56,48},{64,56},{72,6... | collective-permute-start | bytes 786440 | tf_op jit(solution)/shard_map/ppermute | solution.py:60
  12.2 9.3 %collective-permute-start = (bf16[128,512]{1,0:T(8,128)(2,1)S(1)}, bf16[128,512]{1,0:T(8,128)(2,1)S(1)}, u32[]{:S(2)}, u32[]{:S(2)}) collective-permute-start(bf16[128,512]{1,0:T(8,128)(2,1)S(1)} %get-tuple-element.18), channel_id=1, source_target_pairs={{7,0},{0,1},{1,2},{2,3},{3,4},{4,5},{5,6},{6,7},{15,8},{8,9},{9,10... | collective-permute-start | bytes 393224 | tf_op jit(solution)/shard_map/ppermute | solution.py:60
  15.8 9.3 %collective-permute-start.2 = (bf16[128,512]{1,0:T(8,128)(2,1)S(1)}, bf16[128,512]{1,0:T(8,128)(2,1)S(1)}, u32[]{:S(2)}, u32[]{:S(2)}) collective-permute-start(bf16[128,512]{1,0:T(8,128)(2,1)S(1)} %get-tuple-element.19), channel_id=1, source_target_pairs={{15,0},{8,1},{9,2},{10,3},{11,4},{12,5},{13,6},{14,7},{23,8},{16,9... | collective-permute-start | bytes 393224 | tf_op jit(solution)/shard_map/ppermute | solution.py:60
  17.7 8.3 %collective-permute-start.4 = (bf16[128,512]{1,0:T(8,128)(2,1)S(1)}, bf16[128,512]{1,0:T(8,128)(2,1)S(1)}, u32[]{:S(2)}, u32[]{:S(2)}) collective-permute-start(bf16[128,512]{1,0:T(8,128)(2,1)S(1)} %get-tuple-element.20), channel_id=1, source_target_pairs={{9,0},{10,1},{11,2},{12,3},{13,4},{14,5},{15,6},{8,7},{17,8},{18,9... | collective-permute-start | bytes 393224 | tf_op jit(solution)/shard_map/ppermute | solution.py:60
  20.5 5.5 %copy-start.1 = (f32[256,640]{1,0:T(8,128)S(1)}, f32[256,640]{1,0:T(8,128)}, u32[]{:S(2)}) copy-start(f32[256,640]{1,0:T(8,128)} %constant.21) | copy-start | bytes 1966084

commit v4 on v1

--- a/solution.py
+++ b/solution.py
@@ -104,21 +104,24 @@
     rounded = row_sums.astype(jnp.bfloat16).reshape(block_count, 2, patch_count, mode_count)
     rounded = jnp.transpose(rounded, (1, 0, 2, 3)).reshape(2, block_count * patch_count, mode_count)
     local = weighted.reshape(block_count * patch_count, mode_count)
-    first = jnp.stack([jnp.concatenate([local, rounded[q]], axis=0) for q in range(2)])
-    second = jnp.stack(
-        [jnp.concatenate([rounded[0], local], axis=0), jnp.concatenate([rounded[1], -local], axis=0)]
-    )
-    summand = lax.dot_general(
-        first, second, (((1,), (1,)), ((0,), (0,))), preferred_element_type=jnp.float32
+    first = [jnp.concatenate([local, rounded[q]], axis=0) for q in range(2)]
+    second = [jnp.concatenate([rounded[0], local], axis=0), jnp.concatenate([rounded[1], -local], axis=0)]
+    flipped = jnp.stack(
+        [
+            lax.dot_general(second[q], first[q], (((0,), (0,)), ((), ())), preferred_element_type=jnp.float32)
+            for q in range(2)
+        ],
+        axis=1,
     )
     n_ax = lax.axis_size("axial")
     n_ci = lax.axis_size("circ")
+    cols = mode_count // n_ci
     rows = mode_count // n_ax
-    cols = mode_count // n_ci
-    arranged = summand.reshape(2, n_ax, rows, n_ci, cols).transpose(1, 3, 0, 2, 4)
-    arranged = arranged.reshape(n_ax * n_ci, 2, rows, cols)
-    result = lax.psum_scatter(arranged, both, scatter_dimension=0, tiled=True)
-    return result.reshape(2, rows, cols)
+    parts = lax.all_to_all(flipped.reshape(n_ci, cols * 2 * mode_count), "circ", 0, 0, tiled=True)
+    partial_value = parts.reshape(n_ci, cols, 2, n_ax, rows).sum(axis=0)
+    arranged = partial_value.transpose(2, 1, 3, 0).reshape(n_ax, 2 * rows * cols)
+    parts = lax.all_to_all(arranged, "axial", 0, 0, tiled=True)
+    return parts.sum(axis=0).reshape(2, rows, cols)
 
 
 def solution(mesh):

time: 2620 us -> 109 us (0.04)
  waiting for transfers between devices: 2560 us -> 3.92 us
  blocking collectives: 0 us -> 60.9 us
    reduce_scatter x1 -> x0, waiting for transfers between devices: 2560 us -> none  [body(): result = lax.psum_scatter(arranged, both, scatter_dimension=0, tiled=True)]
    all_to_all x0 -> x2, blocking collectives: none -> 60.9 us  [the longest x1 35.6 us: body(): lax.all_to_all(flipped.reshape(n_ci, cols * 2 * mode_count), 'circ', 0, 0...]
  transfers between devices with their start and end apart: 6 -> 5, of which waited for: 3 -> 2; matrix products, arithmetic and copies ran while one was open for 0% -> 0% of each run, Pallas kernels for 0% -> 0%
where the time goes in v4:
time: 109 us; the launch traced here: 108 us
  blocking collectives  60.9 us (56%)
  starting transfers between devices  19.9 us (18%)
  local copies, waits for them, and re-layouts  16.4 us (15%)
  waiting for transfers between devices  3.92 us (4%)
  other arithmetic  3.33 us (3%)
  matrix products  2.62 us (2%)
    all_to_all x1, blocking collectives, body(): lax.all_to_all(flipped.reshape(n_ci, cols * 2 * mode_count), 'circ', 0, 0...  35.6 us
    all_to_all x1, blocking collectives, body(): parts = lax.all_to_all(arranged, 'axial', 0, 0, tiled=True)  25.3 us
    ppermute x5, starting transfers between devices, shifted(): return lax.ppermute(block, axes if len(axes) > 1 else axes[0], pairs)  19.9 us
    all_to_all x1, local copies, waits for them, and re-layouts, body(): lax.all_to_all(flipped.reshape(n_ci, cols * 2 * mode_count), 'circ', 0, 0...  4.87 us
    transpose x1, local copies, waits for them, and re-layouts, body(): partial_value.transpose(2, 1, 3, 0).reshape(n_ax, 2 * rows * cols)  4.85 us
    ppermute x5, waiting for transfers between devices, shifted(): return lax.ppermute(block, axes if len(axes) > 1 else axes[0], pairs)  3.92 us
    reduce_sum x1, local copies, waits for them, and re-layouts, body(): partial_value = parts.reshape(n_ci, cols, 2, n_ax, rows).sum(axis=0)  3.62 us
  transfers between devices with their start and end apart: 5, of which 2 were waited for; matrix products, arithmetic and copies ran while one was open for 0% of the time, Pallas kernels for 0%

profile of v4, /device:TPU:1, one launch (start us, length us, event | category | flops | bytes accessed | tf_op | source)
XLA Modules:
  0.0 108.0 jit_solution(7822955144293452200)
XLA Ops:
  0.0 1.4 %multiply_convert_fusion.2 = bf16[2,2,128,512]{3,2,1,0:T(8,128)(2,1)S(1)} fusion(f32[2,2,128,512]{3,2,1,0:T(8,128)} %param.5, f32[2,2,128]{2,1,0:T(2,128)} %param.6), kind=kLoop, calls=%fused_computation.25 | loop fusion | flops 524288 | bytes 1574912 | tf_op jit(solution)/shard_map/convert_element_type | solution.py:58
  1.4 4.0 %collective-permute-start = (bf16[128,512]{1,0:T(8,128)(2,1)S(1)}, bf16[128,512]{1,0:T(8,128)(2,1)S(1)}, u32[]{:S(2)}, u32[]{:S(2)}) collective-permute-start(bf16[128,512]{1,0:T(8,128)(2,1)S(1)} %get-tuple-element.14), channel_id=1, source_target_pairs={{7,0},{0,1},{1,2},{2,3},{3,4},{4,5},{5,6},{6,7},{15,8},{8,9},{9,10... | collective-permute-start | bytes 393224 | tf_op jit(solution)/shard_map/ppermute | solution.py:52
  5.5 4.1 %collective-permute-start.1 = (bf16[2,128,512]{2,1,0:T(8,128)(2,1)S(1)}, bf16[2,128,512]{2,1,0:T(8,128)(2,1)S(1)}, u32[]{:S(2)}, u32[]{:S(2)}) collective-permute-start(bf16[2,128,512]{2,1,0:T(8,128)(2,1)S(1)} %slice_bitcast_fusion.1), channel_id=1, source_target_pairs={{1,0},{2,1},{3,2},{4,3},{5,4},{6,5},{7,6},{0,7},{9,8},{10,9},{11,1... | collective-permute-start | bytes 786440 | tf_op jit(solution)/shard_map/ppermute | solution.py:52
  9.6 6.1 %collective-permute-start.2 = (bf16[128,512]{1,0:T(8,128)(2,1)S(1)}, bf16[128,512]{1,0:T(8,128)(2,1)S(1)}, u32[]{:S(2)}, u32[]{:S(2)}) collective-permute-start(bf16[128,512]{1,0:T(8,128)(2,1)S(1)} %get-tuple-element.15), channel_id=1, source_target_pairs={{15,0},{8,1},{9,2},{10,3},{11,4},{12,5},{13,6},{14,7},{23,8},{16,9... | collective-permute-start | bytes 393224 | tf_op jit(solution)/shard_map/ppermute | solution.py:52
  15.7 3.8 %collective-permute-start.3 = (bf16[2,128,512]{2,1,0:T(8,128)(2,1)S(1)}, bf16[2,128,512]{2,1,0:T(8,128)(2,1)S(1)}, u32[]{:S(2)}, u32[]{:S(2)}) collective-permute-start(bf16[2,128,512]{2,1,0:T(8,128)(2,1)S(1)} %slice_bitcast_fusion), channel_id=1, source_target_pairs={{8,0},{16,8},{24,16},{32,24},{40,32},{48,40},{56,48},{64,56},{72,6... | collective-permute-start | bytes 786440 | tf_op jit(solution)/shard_map/ppermute | solution.py:52
  19.5 1.9 %collective-permute-start.4 = (bf16[128,512]{1,0:T(8,128)(2,1)S(1)}, bf16[128,512]{1,0:T(8,128)(2,1)S(1)}, u32[]{:S(2)}, u32[]{:S(2)}) collective-permute-start(bf16[128,512]{1,0:T(8,128)(2,1)S(1)} %get-tuple-element.16), channel_id=1, source_target_pairs={{9,0},{10,1},{11,2},{12,3},{13,4},{14,5},{15,6},{8,7},{17,8},{18,9... | collective-permute-start | bytes 393224 | tf_op jit(solution)/shard_map/ppermute | solution.py:52
  22.3 0.1 fusion.31
  22.4 0.1 broadcast_bitcast_fusion
  22.7 1.0 collective-permute-done.3
  23.7 2.9 %collective-permute-done.4 = bf16[128,512]{1,0:T(8,128)(2,1)S(1)} collective-permute-done((bf16[128,512]{1,0:T(8,128)(2,1)S(1)}, bf16[128,512]{1,0:T(8,128)(2,1)S(1)}, u32[]{:S(2)}, u32[]{:S(2)}) %collective-permute-start.4) | collective-permute-done | bytes 131104 | tf_op jit(solution)/shard_map/ppermute | solution.py:52
  26.7 1.0 fusion.8
  27.8 0.7 convolution_bitcast_fusion.1
  28.6 0.7 convolution_bitcast_fusion
  29.3 0.2 pad_maximum_fusion
  29.5 1.6 %copy.8 = f32[512,2,512]{2,1,0:T(2,128)S(1)} copy(f32[512,2,512]{2,0,1:T(8,128)S(1)} %pad_maximum_fusion) | data formatting | bytes 4194304 | tf_op jit(solution)/shard_map/stack | solution.py:109
  31.1 4.9 %all_to_all.16 = f32[8,1,65536]{2,1,0:T(1,128)} reshape(f32[512,2,512]{2,1,0:T(2,128)S(1)} %copy.8) | data formatting | bytes 4194304 | tf_op jit(solution)/shard_map/all_to_all | solution.py:120
  36.0 35.6 %all_to_all.20 = f32[8,1,65536]{2,1,0:T(1,128)S(1)} all-to-all(f32[8,1,65536]{2,1,0:T(1,128)} %all_to_all.16), channel_id=1, replica_groups=mesh['axial'=64,'circ'=8] {'circ'}, dimensions={0} | all-to-all | bytes 4194304 | tf_op jit(solution)/shard_map/all_to_all | solution.py:120
  71.5 1.5 %reduce_sum.20 = f32[65536]{0:T(1024)S(1)} reduce(f32[8,1,65536]{2,1,0:T(1,128)S(1)} %all_to_all.20, f32[]{:T(128)} %constant.13.clone.1), dimensions={0,1}, to_apply=%region_0.1 | reduce | flops 458752 | bytes 2359300 | tf_op jit(solution)/shard_map/reduce_sum | solution.py:121
  73.1 3.6 %reduce_sum.21 = f32[64,2,64,8]{3,2,1,0:T(8,128)} reshape(f32[65536]{0:T(1024)S(1)} %reduce_sum.20) | data formatting | bytes 524288 | tf_op jit(solution)/shard_map/reduce_sum | solution.py:121
  76.7 4.8 %copy.10 = f32[64,2,8,64]{3,2,1,0:T(8,128)S(1)} copy(f32[64,2,8,64]{2,0,1,3:T(8,128)} %bitcast.85) | data formatting | bytes 524288 | tf_op jit(solution)/shard_map/transpose | solution.py:122
  81.5 0.3 all_to_all.17
  81.9 25.3 %all_to_all.21 = f32[64,1,1024]{2,1,0:T(1,128)S(1)} all-to-all(f32[64,1,1024]{2,1,0:T(1,128)S(1)} %all_to_all.17), channel_id=1, replica_groups=mesh['axial'=64,'circ'=8] {'axial'}, dimensions={0} | all-to-all | bytes 524288 | tf_op jit(solution)/shard_map/all_to_all | solution.py:123
  107.2 0.2 reduce_sum.22
  107.4 0.7 reshape.60
  (27 shorter events, 0.4 us)
Async XLA Ops:
  0.0 21.5 %copy-start = (s32[1,1,3,20]{3,1,2,0:T(1,128)S(1)}, s32[1,1,3,20]{3,1,2,0:T(1,128)}, u32[]{:S(2)}) copy-start(s32[1,1,3,20]{3,1,2,0:T(1,128)} %param.7) | copy-start | bytes 724
  1.4 21.1 %collective-permute-start = (bf16[128,512]{1,0:T(8,128)(2,1)S(1)}, bf16[128,512]{1,0:T(8,128)(2,1)S(1)}, u32[]{:S(2)}, u32[]{:S(2)}) collective-permute-start(bf16[128,512]{1,0:T(8,128)(2,1)S(1)} %get-tuple-element.14), channel_id=1, source_target_pairs={{7,0},{0,1},{1,2},{2,3},{3,4},{4,5},{5,6},{6,7},{15,8},{8,9},{9,10... | collective-permute-start | bytes 393224 | tf_op jit(solution)/shard_map/ppermute | solution.py:52
  5.5 17.1 %collective-permute-start.1 = (bf16[2,128,512]{2,1,0:T(8,128)(2,1)S(1)}, bf16[2,128,512]{2,1,0:T(8,128)(2,1)S(1)}, u32[]{:S(2)}, u32[]{:S(2)}) collective-permute-start(bf16[2,128,512]{2,1,0:T(8,128)(2,1)S(1)} %slice_bitcast_fusion.1), channel_id=1, source_target_pairs={{1,0},{2,1},{3,2},{4,3},{5,4},{6,5},{7,6},{0,7},{9,8},{10,9},{11,1... | collective-permute-start | bytes 786440 | tf_op jit(solution)/shard_map/ppermute | solution.py:52
  9.6 13.1 %collective-permute-start.2 = (bf16[128,512]{1,0:T(8,128)(2,1)S(1)}, bf16[128,512]{1,0:T(8,128)(2,1)S(1)}, u32[]{:S(2)}, u32[]{:S(2)}) collective-permute-start(bf16[128,512]{1,0:T(8,128)(2,1)S(1)} %get-tuple-element.15), channel_id=1, source_target_pairs={{15,0},{8,1},{9,2},{10,3},{11,4},{12,5},{13,6},{14,7},{23,8},{16,9... | collective-permute-start | bytes 393224 | tf_op jit(solution)/shard_map/ppermute | solution.py:52
  15.7 8.0 %collective-permute-start.3 = (bf16[2,128,512]{2,1,0:T(8,128)(2,1)S(1)}, bf16[2,128,512]{2,1,0:T(8,128)(2,1)S(1)}, u32[]{:S(2)}, u32[]{:S(2)}) collective-permute-start(bf16[2,128,512]{2,1,0:T(8,128)(2,1)S(1)} %slice_bitcast_fusion), channel_id=1, source_target_pairs={{8,0},{16,8},{24,16},{32,24},{40,32},{48,40},{56,48},{64,56},{72,6... | collective-permute-start | bytes 786440 | tf_op jit(solution)/shard_map/ppermute | solution.py:52
  19.5 7.2 %collective-permute-start.4 = (bf16[128,512]{1,0:T(8,128)(2,1)S(1)}, bf16[128,512]{1,0:T(8,128)(2,1)S(1)}, u32[]{:S(2)}, u32[]{:S(2)}) collective-permute-start(bf16[128,512]{1,0:T(8,128)(2,1)S(1)} %get-tuple-element.16), channel_id=1, source_target_pairs={{9,0},{10,1},{11,2},{12,3},{13,4},{14,5},{15,6},{8,7},{17,8},{18,9... | collective-permute-start | bytes 393224 | tf_op jit(solution)/shard_map/ppermute | solution.py:52
  21.5 5.2 %copy-start.1 = (f32[256,640]{1,0:T(8,128)S(1)}, f32[256,640]{1,0:T(8,128)}, u32[]{:S(2)}) copy-start(f32[256,640]{1,0:T(8,128)} %constant.21) | copy-start | bytes 1966084

commit v5 on v3

--- a/solution.py
+++ b/solution.py
@@ -112,22 +112,29 @@
     rounded = row_sums.astype(jnp.bfloat16).reshape(block_count, 2, patch_count, mode_count)
     rounded = jnp.transpose(rounded, (1, 0, 2, 3)).reshape(2, block_count * patch_count, mode_count)
     local = weighted.reshape(block_count * patch_count, mode_count)
-    first = jnp.stack([jnp.concatenate([local, rounded[q]], axis=0) for q in range(2)])
-    second = jnp.stack(
-        [jnp.concatenate([rounded[0], local], axis=0), jnp.concatenate([rounded[1], -local], axis=0)]
-    )
-    summand = lax.dot_general(
-        first, second, (((1,), (1,)), ((0,), (0,))), preferred_element_type=jnp.float32
-    )
     n_core = lax.axis_size("core")
     outer = group_size(AXIAL) // n_core
     n_ci = group_size(CIRC)
     cols = mode_count // n_ci
     rows = mode_count // (outer * n_core)
-    arranged = summand.reshape(2, outer, n_core, rows, n_ci, cols).transpose(4, 2, 1, 0, 3, 5)
-    arranged = arranged.reshape(n_ci * n_core, outer * 2 * rows * cols)
-    parts = lax.all_to_all(arranged, CIRC + ("core",), 0, 0, tiled=True)
-    partial_value = parts.reshape(n_ci * n_core, outer, 2 * rows * cols).sum(axis=0)
+    first = jnp.concatenate([local, rounded[0], rounded[1]], axis=0)
+    first = first.reshape(-1, outer, n_core, rows).transpose(0, 2, 1, 3).reshape(first.shape[0], mode_count)
+    zeros = jnp.zeros_like(local)
+    second = jnp.concatenate(
+        [
+            jnp.concatenate([rounded[0], local, zeros], axis=0),
+            jnp.concatenate([rounded[1], zeros, -local], axis=0),
+        ],
+        axis=1,
+    )
+    summand = lax.dot_general(
+        first, second, (((0,), (0,)), ((), ())), preferred_element_type=jnp.float32
+    )
+    parts = lax.all_to_all(summand.reshape(n_core, -1), "core", 0, 0, tiled=True)
+    halves = parts.reshape(n_core, outer, rows, 2, n_ci, cols).sum(axis=0)
+    arranged = halves.transpose(3, 0, 2, 1, 4).reshape(n_ci, -1)
+    parts = lax.all_to_all(arranged, CIRC, 0, 0, tiled=True)
+    partial_value = parts.reshape(n_ci, outer, -1).sum(axis=0)
     parts = lax.all_to_all(partial_value, AXIAL[:-1], 0, 0, tiled=True)
     return parts.sum(axis=0).reshape(2, rows, cols)
 

time: 105 us -> 126 us (1.20)
  matrix products: 2.45 us -> 16.3 us
  other arithmetic: 4.94 us -> 15 us
  local copies, waits for them, and re-layouts: 13 us -> 18.9 us
  blocking collectives: 59.8 us -> 53.9 us
  waiting for transfers between devices: 4.28 us -> 0.01 us
    dot_general x1, matrix products: 1.3 us -> 14 us  [body(): lax.dot_general(first, second, (((0,), (0,)), ((), ())), preferred_elemen...]
    reduce_sum x1 -> x2, other arithmetic: 2.95 us -> 12.5 us  [the longest x1 11.8 us: body(): halves = parts.reshape(n_core, outer, rows, 2, n_ci, cols).sum(axis=0)]
    reshape x2 -> x1, local copies, waits for them, and re-layouts: 7.36 us -> 0.75 us  [body(): row_sums.astype(jnp.bfloat16)]
    all_to_all x1 -> x2, blocking collectives: 33.5 us -> 29 us  [the longest x1 22.9 us: body(): parts = lax.all_to_all(arranged, CIRC, 0, 0, tiled=True)]
    ppermute x5, waiting for transfers between devices: 4.28 us -> 0.01 us  [shifted(): return lax.ppermute(block, sum(axes, ()), pairs)]
    unnamed x14 -> x18, local copies, waits for them, and re-layouts: 0.2 us -> 3.83 us
    transpose x0 -> x2, local copies, waits for them, and re-layouts: none -> 2.09 us  [the longest x1 1.99 us: body(): arranged = halves.transpose(3, 0, 2, 1, 4).reshape(n_ci, -1)]
    all_to_all x1 -> x2, local copies, waits for them, and re-layouts: 4.52 us -> 6.3 us  [the longest x1 3.75 us: body(): lax.all_to_all(summand.reshape(n_core, -1), 'core', 0, 0, tiled=True)]
  transfers between devices with their start and end apart: 5 -> 5, of which waited for: 2 -> 0; matrix products, arithmetic and copies ran while one was open for 0% -> 4% of each run, Pallas kernels for 0% -> 0%
where the time goes in v5:
time: 126 us; the launch traced here: 125 us
  blocking collectives  53.9 us (43%)
  starting transfers between devices  19.9 us (16%)
  local copies, waits for them, and re-layouts  18.9 us (15%)
  matrix products  16.3 us (13%)
  other arithmetic  15 us (12%)
    all_to_all x1, blocking collectives, body(): parts = lax.all_to_all(partial_value, AXIAL[:-1], 0, 0, tiled=True)  24.9 us
    all_to_all x1, blocking collectives, body(): parts = lax.all_to_all(arranged, CIRC, 0, 0, tiled=True)  22.9 us
    ppermute x5, starting transfers between devices, shifted(): return lax.ppermute(block, sum(axes, ()), pairs)  19.9 us
    dot_general x1, matrix products, body(): lax.dot_general(first, second, (((0,), (0,)), ((), ())), preferred_elemen...  14 us
    reduce_sum x1, other arithmetic, body(): halves = parts.reshape(n_core, outer, rows, 2, n_ci, cols).sum(axis=0)  11.8 us
    all_to_all x1, blocking collectives, body(): lax.all_to_all(summand.reshape(n_core, -1), 'core', 0, 0, tiled=True)  6.17 us
    unnamed x18, local copies, waits for them, and re-layouts  3.83 us
    all_to_all x1, local copies, waits for them, and re-layouts, body(): lax.all_to_all(summand.reshape(n_core, -1), 'core', 0, 0, tiled=True)  3.75 us
  transfers between devices with their start and end apart: 5, of which 0 were waited for; matrix products, arithmetic and copies ran while one was open for 4% of the time, Pallas kernels for 0%

profile of v5, /device:TPU:1, one launch (start us, length us, event | category | flops | bytes accessed | tf_op | source)
XLA Modules:
  0.0 124.9 jit_solution(5907577750999362169)
XLA Ops:
  0.0 1.4 %multiply_convert_fusion.2 = bf16[2,2,128,512]{3,2,1,0:T(8,128)(2,1)S(1)} fusion(f32[2,2,128,512]{3,2,1,0:T(8,128)} %param.5, f32[2,2,128]{2,1,0:T(2,128)} %param.6), kind=kLoop, calls=%fused_computation.25 | loop fusion | flops 524288 | bytes 1574912 | tf_op jit(solution)/shard_map/convert_element_type | solution.py:66
  1.4 4.0 %collective-permute-start = (bf16[128,512]{1,0:T(8,128)(2,1)S(1)}, bf16[128,512]{1,0:T(8,128)(2,1)S(1)}, u32[]{:S(2)}, u32[]{:S(2)}) collective-permute-start(bf16[128,512]{1,0:T(8,128)(2,1)S(1)} %get-tuple-element.14), channel_id=1, source_target_pairs={{7,0},{0,1},{1,2},{2,3},{3,4},{4,5},{5,6},{6,7},{15,8},{8,9},{9,10... | collective-permute-start | bytes 393224 | tf_op jit(solution)/shard_map/ppermute | solution.py:60
  5.5 4.1 %collective-permute-start.1 = (bf16[2,128,512]{2,1,0:T(8,128)(2,1)S(1)}, bf16[2,128,512]{2,1,0:T(8,128)(2,1)S(1)}, u32[]{:S(2)}, u32[]{:S(2)}) collective-permute-start(bf16[2,128,512]{2,1,0:T(8,128)(2,1)S(1)} %slice_bitcast_fusion.1), channel_id=1, source_target_pairs={{1,0},{2,1},{3,2},{4,3},{5,4},{6,5},{7,6},{0,7},{9,8},{10,9},{11,1... | collective-permute-start | bytes 786440 | tf_op jit(solution)/shard_map/ppermute | solution.py:60
  9.6 6.1 %collective-permute-start.2 = (bf16[128,512]{1,0:T(8,128)(2,1)S(1)}, bf16[128,512]{1,0:T(8,128)(2,1)S(1)}, u32[]{:S(2)}, u32[]{:S(2)}) collective-permute-start(bf16[128,512]{1,0:T(8,128)(2,1)S(1)} %get-tuple-element.15), channel_id=1, source_target_pairs={{15,0},{8,1},{9,2},{10,3},{11,4},{12,5},{13,6},{14,7},{23,8},{16,9... | collective-permute-start | bytes 393224 | tf_op jit(solution)/shard_map/ppermute | solution.py:60
  15.7 3.8 %collective-permute-start.3 = (bf16[2,128,512]{2,1,0:T(8,128)(2,1)S(1)}, bf16[2,128,512]{2,1,0:T(8,128)(2,1)S(1)}, u32[]{:S(2)}, u32[]{:S(2)}) collective-permute-start(bf16[2,128,512]{2,1,0:T(8,128)(2,1)S(1)} %slice_bitcast_fusion), channel_id=1, source_target_pairs={{8,0},{16,8},{24,16},{32,24},{40,32},{48,40},{56,48},{64,56},{72,6... | collective-permute-start | bytes 786440 | tf_op jit(solution)/shard_map/ppermute | solution.py:60
  19.5 1.9 %collective-permute-start.4 = (bf16[128,512]{1,0:T(8,128)(2,1)S(1)}, bf16[128,512]{1,0:T(8,128)(2,1)S(1)}, u32[]{:S(2)}, u32[]{:S(2)}) collective-permute-start(bf16[128,512]{1,0:T(8,128)(2,1)S(1)} %get-tuple-element.16), channel_id=1, source_target_pairs={{9,0},{10,1},{11,2},{12,3},{13,4},{14,5},{15,6},{8,7},{17,8},{18,9... | collective-permute-start | bytes 393224 | tf_op jit(solution)/shard_map/ppermute | solution.py:60
  22.5 0.9 bitcast_negate_fusion
  25.8 0.7 fusion.34
  26.5 0.7 constant_dynamic-update-slice_fusion
  27.3 2.1 %fusion.20 = bf16[4,256,512]{2,1,0:T(8,128)(2,1)S(1)} fusion(bf16[1,640,512]{2,1,0:T(8,128)(2,1)S(1)} %bitcast.99, bf16[1,640,512]{2,1,0:T(8,128)(2,1)S(1)} %bitcast.100, bf16[1,640,512]{2,1,0:T(8,128)(2,1)S(1)} %bitcast.101, bf16[1,640,512]{2,1,0:T(8,128)(2,1)} %bitcast.102, f32[4,640]{1,0:T(4,128)S(1)} %bitcast.103, f32[256,640]{1,0:T(8,128)S(1)} %copy-done.3), kind=kOutput, calls=%fused_computation.22 | convolution fusion | flops 676855808 | bytes 4335616 | tf_op jit(solution)/shard_map/dot_general | solution.py:109
  29.4 0.8 copy.34
  31.3 1.1 copy.43
  32.7 0.9 copy-done
  33.7 14.0 %fusion = f32[512,1024]{1,0:T(8,128)} fusion(bf16[1536,512]{0,1:T(8,128)(2,1)S(1)} %bitcast.94, bf16[512,512]{1,0:T(8,128)(2,1)S(1)} %copy-done, bf16[512,512]{1,0:T(8,128)(2,1)S(1)} %broadcast_in_dim.19, bf16[512,512]{1,0:T(8,128)(2,1)S(1)} %bitcast.98, bf16[512,512]{1,0:T(8,128)(2,1)S(1)} %bitcast.91, bf16[512,512]{1,0:T(8,128)(2,1)S(1)} %bitcast.97), kind=kOutput, calls=%fused_computation | convolution fusion | flops 1629487104 | bytes 6291456 | tf_op jit(solution)/shard_map/dot_general | solution.py:130
  47.8 3.7 %all_to_all.24 = f32[2,1,262144]{2,1,0:T(1,128)S(1)} reshape(f32[512,1024]{1,0:T(8,128)} %fusion) | data formatting | bytes 4194304 | tf_op jit(solution)/shard_map/all_to_all | solution.py:133
  51.5 6.2 %all_to_all.29 = f32[2,1,262144]{2,1,0:T(1,128)} all-to-all(f32[2,1,262144]{2,1,0:T(1,128)S(1)} %all_to_all.24), channel_id=1, replica_groups=mesh['y_hi'=4,'z'=8,'core'=2,'x'=4,'y_lo'=2] {'core'}, dimensions={0} | all-to-all | bytes 4194304 | tf_op jit(solution)/shard_map/all_to_all | solution.py:133
  57.7 11.8 %reduce_sum.29 = f32[262144]{0:T(1024)} reduce(f32[2,1,262144]{2,1,0:T(1,128)} %all_to_all.29, f32[]{:T(128)} %constant.14.clone.1), dimensions={0,1}, to_apply=%region_0.1 | reduce | flops 262144 | bytes 3145732 | tf_op jit(solution)/shard_map/reduce_sum | solution.py:134
  69.5 1.6 %reduce_sum.30 = f32[32,8,2,8,64]{4,3,2,1,0:T(8,128)S(1)} reshape(f32[262144]{0:T(1024)} %reduce_sum.29) | data formatting | bytes 2097152 | tf_op jit(solution)/shard_map/reduce_sum | solution.py:134
  71.1 2.0 %copy.39 = f32[8,32,2,8,64]{4,3,2,1,0:T(8,128)} copy(f32[8,32,2,8,64]{4,0,2,3,1:T(8,128)S(1)} %bitcast.92) | data formatting | bytes 2097152 | tf_op jit(solution)/shard_map/transpose | solution.py:135
  73.0 2.6 %all_to_all.25 = f32[8,1,32768]{2,1,0:T(1,128)S(1)} reshape(f32[8,32,2,8,64]{4,3,2,1,0:T(8,128)} %copy.39) | data formatting | bytes 2097152 | tf_op jit(solution)/shard_map/all_to_all | solution.py:136
  75.6 22.9 %all_to_all.30 = f32[8,1,32768]{2,1,0:T(1,128)S(1)} all-to-all(f32[8,1,32768]{2,1,0:T(1,128)S(1)} %all_to_all.25), channel_id=1, replica_groups=mesh['y_hi'=4,'z'=8,'core'=2,'x'=4,'y_lo'=2] {'x','y_lo'}, dimensions={0} | all-to-all | bytes 2097152 | tf_op jit(solution)/shard_map/all_to_all | solution.py:136
  98.5 0.8 reduce_sum.31
  99.2 24.9 %all_to_all.31 = f32[32,1,1024]{2,1,0:T(1,128)S(1)} all-to-all(f32[32,1,1024]{2,1,0:T(1,128)S(1)} %bitcast.96), channel_id=1, replica_groups=mesh['y_hi'=4,'z'=8,'core'=2,'x'=4,'y_lo'=2] {'y_hi','z'}, dimensions={0} | all-to-all | bytes 262144 | tf_op jit(solution)/shard_map/all_to_all | solution.py:138
  124.2 0.7 reshape.76
  (40 shorter events, 4.6 us)
Async XLA Ops:
  1.4 22.0 %copy-start.2 = (s32[1,1,3,20]{3,1,2,0:T(1,128)S(1)}, s32[1,1,3,20]{3,1,2,0:T(1,128)}, u32[]{:S(2)}) copy-start(s32[1,1,3,20]{3,1,2,0:T(1,128)} %param.7) | copy-start | bytes 724
  1.4 23.7 %collective-permute-start = (bf16[128,512]{1,0:T(8,128)(2,1)S(1)}, bf16[128,512]{1,0:T(8,128)(2,1)S(1)}, u32[]{:S(2)}, u32[]{:S(2)}) collective-permute-start(bf16[128,512]{1,0:T(8,128)(2,1)S(1)} %get-tuple-element.14), channel_id=1, source_target_pairs={{7,0},{0,1},{1,2},{2,3},{3,4},{4,5},{5,6},{6,7},{15,8},{8,9},{9,10... | collective-permute-start | bytes 393224 | tf_op jit(solution)/shard_map/ppermute | solution.py:60
  5.5 21.0 %collective-permute-start.1 = (bf16[2,128,512]{2,1,0:T(8,128)(2,1)S(1)}, bf16[2,128,512]{2,1,0:T(8,128)(2,1)S(1)}, u32[]{:S(2)}, u32[]{:S(2)}) collective-permute-start(bf16[2,128,512]{2,1,0:T(8,128)(2,1)S(1)} %slice_bitcast_fusion.1), channel_id=1, source_target_pairs={{1,0},{2,1},{3,2},{4,3},{5,4},{6,5},{7,6},{0,7},{9,8},{10,9},{11,1... | collective-permute-start | bytes 786440 | tf_op jit(solution)/shard_map/ppermute | solution.py:60
  9.6 17.6 %collective-permute-start.2 = (bf16[128,512]{1,0:T(8,128)(2,1)S(1)}, bf16[128,512]{1,0:T(8,128)(2,1)S(1)}, u32[]{:S(2)}, u32[]{:S(2)}) collective-permute-start(bf16[128,512]{1,0:T(8,128)(2,1)S(1)} %get-tuple-element.15), channel_id=1, source_target_pairs={{15,0},{8,1},{9,2},{10,3},{11,4},{12,5},{13,6},{14,7},{23,8},{16,9... | collective-permute-start | bytes 393224 | tf_op jit(solution)/shard_map/ppermute | solution.py:60
  15.7 11.5 %collective-permute-start.3 = (bf16[2,128,512]{2,1,0:T(8,128)(2,1)S(1)}, bf16[2,128,512]{2,1,0:T(8,128)(2,1)S(1)}, u32[]{:S(2)}, u32[]{:S(2)}) collective-permute-start(bf16[2,128,512]{2,1,0:T(8,128)(2,1)S(1)} %slice_bitcast_fusion), channel_id=1, source_target_pairs={{8,0},{16,8},{24,16},{32,24},{40,32},{48,40},{56,48},{64,56},{72,6... | collective-permute-start | bytes 786440 | tf_op jit(solution)/shard_map/ppermute | solution.py:60
  19.5 7.8 %collective-permute-start.4 = (bf16[128,512]{1,0:T(8,128)(2,1)S(1)}, bf16[128,512]{1,0:T(8,128)(2,1)S(1)}, u32[]{:S(2)}, u32[]{:S(2)}) collective-permute-start(bf16[128,512]{1,0:T(8,128)(2,1)S(1)} %get-tuple-element.16), channel_id=1, source_target_pairs={{9,0},{10,1},{11,2},{12,3},{13,4},{14,5},{15,6},{8,7},{17,8},{18,9... | collective-permute-start | bytes 393224 | tf_op jit(solution)/shard_map/ppermute | solution.py:60
  24.4 2.9 %copy-start.3 = (f32[256,640]{1,0:T(8,128)S(1)}, f32[256,640]{1,0:T(8,128)}, u32[]{:S(2)}) copy-start(f32[256,640]{1,0:T(8,128)} %constant.23) | copy-start | bytes 1966084
  32.5 1.0 copy-start
  32.5 1.2 copy-start.1

commit v6 on v2

--- a/solution.py
+++ b/solution.py
@@ -59,23 +59,18 @@
 
     both = ("axial", "circ")
     right = shifted(weighted[:, 0], ("circ",), ((1, True),))
-    left = shifted(weighted[1, 1], ("circ",), ((-1, True),))
-    ahead = shifted(weighted[0], ("axial",), ((1, False),))
-    ahead_left = shifted(weighted[0, 1], both, ((1, False), (-1, True)))
-    ahead_right = shifted(weighted[0, 0], both, ((1, False), (1, True)))
+    left = shifted(weighted[:, 1], ("circ",), ((-1, True),))
+    widened = jnp.stack([left[0], weighted[0, 0], weighted[0, 1], right[0]])
+    ahead = shifted(widened, ("axial",), ((1, False),))
 
     def window(x, y):
         if x < 2 and 0 <= y < 2:
             return weighted[x, y]
         if x < 2 and y == 2:
             return right[x]
-        if x == 1 and y == -1:
-            return left
-        if x == 2 and 0 <= y < 2:
-            return ahead[y]
-        if x == 2 and y == -1:
-            return ahead_left
-        return ahead_right
+        if x < 2 and y == -1:
+            return left[x]
+        return ahead[y + 1]
 
     columns = jnp.stack(
         [

time: 96 us -> 96.9 us (level)
  waiting for transfers between devices: 0.56 us -> 14.2 us
  starting transfers between devices: 19.9 us -> 13 us
  local copies, waits for them, and re-layouts: 5.76 us -> 2.51 us
  blocking collectives: 60.7 us -> 59.3 us
  matrix products: 3.51 us -> 2.41 us
    ppermute x5 -> x3, waiting for transfers between devices: 0.56 us -> 14.2 us  [shifted(): return lax.ppermute(block, axes if len(axes) > 1 else axes[0], pairs)]
    ppermute x5 -> x3, starting transfers between devices: 19.9 us -> 13 us  [shifted(): return lax.ppermute(block, axes if len(axes) > 1 else axes[0], pairs)]
    all_to_all x1, blocking collectives: 35.3 us -> 30.6 us  [body(): lax.all_to_all(summand.reshape(2, mode_count, n_ci, cols), 'circ', 2, 0,...]
    all_to_all x1, blocking collectives: 25.3 us -> 28.7 us  [body(): lax.all_to_all(partial_value.reshape(2, n_ax, rows, cols), 'axial', 1, 0,...]
    unnamed x17, local copies, waits for them, and re-layouts: 3.31 us -> 0.7 us
    dot_general x1, matrix products: 2.1 us -> 1 us  [body(): lax.dot_general(lhs, columns, (((2,), (1,)), ((0,), (0,))), preferred_ele...]
  transfers between devices with their start and end apart: 5 -> 3, of which waited for: 1 -> 3; matrix products, arithmetic and copies ran while one was open for 4% -> 1% of each run, Pallas kernels for 0% -> 0%
where the time goes in v6:
time: 96.9 us; the launch traced here: 96.7 us
  blocking collectives  59.3 us (61%)
  waiting for transfers between devices  14.2 us (15%)
  starting transfers between devices  13 us (13%)
  other arithmetic  4.24 us (4%)
  local copies, waits for them, and re-layouts  2.51 us (3%)
  matrix products  2.41 us (2%)
    all_to_all x1, blocking collectives, body(): lax.all_to_all(summand.reshape(2, mode_count, n_ci, cols), 'circ', 2, 0,...  30.6 us
    all_to_all x1, blocking collectives, body(): lax.all_to_all(partial_value.reshape(2, n_ax, rows, cols), 'axial', 1, 0,...  28.7 us
    ppermute x3, waiting for transfers between devices, shifted(): return lax.ppermute(block, axes if len(axes) > 1 else axes[0], pairs)  14.2 us
    ppermute x3, starting transfers between devices, shifted(): return lax.ppermute(block, axes if len(axes) > 1 else axes[0], pairs)  13 us
  transfers between devices with their start and end apart: 3, of which 3 were waited for; matrix products, arithmetic and copies ran while one was open for 1% of the time, Pallas kernels for 0%

profile of v6, /device:TPU:1, one launch (start us, length us, event | category | flops | bytes accessed | tf_op | source)
XLA Modules:
  0.0 96.7 jit_solution(12569277020860887650)
XLA Ops:
  0.0 1.4 %multiply_convert_fusion.2 = bf16[2,2,128,512]{3,2,1,0:T(8,128)(2,1)S(1)} fusion(f32[2,2,128,512]{3,2,1,0:T(8,128)} %param.5, f32[2,2,128]{2,1,0:T(2,128)} %param.6), kind=kLoop, calls=%fused_computation.25 | loop fusion | flops 524288 | bytes 1574912 | tf_op jit(solution)/shard_map/convert_element_type | solution.py:58
  1.4 4.0 %collective-permute-start = (bf16[2,128,512]{2,1,0:T(8,128)(2,1)S(1)}, bf16[2,128,512]{2,1,0:T(8,128)(2,1)S(1)}, u32[]{:S(2)}, u32[]{:S(2)}) collective-permute-start(bf16[2,128,512]{2,1,0:T(8,128)(2,1)S(1)} %get-tuple-element.22), channel_id=1, source_target_pairs={{7,0},{0,1},{1,2},{2,3},{3,4},{4,5},{5,6},{6,7},{15,8},{8,9},{9,10... | collective-permute-start | bytes 786440 | tf_op jit(solution)/shard_map/ppermute | solution.py:52
  5.5 4.1 %collective-permute-start.1 = (bf16[2,128,512]{2,1,0:T(8,128)(2,1)S(1)}, bf16[2,128,512]{2,1,0:T(8,128)(2,1)S(1)}, u32[]{:S(2)}, u32[]{:S(2)}) collective-permute-start(bf16[2,128,512]{2,1,0:T(8,128)(2,1)S(1)} %get-tuple-element.23), channel_id=1, source_target_pairs={{1,0},{2,1},{3,2},{4,3},{5,4},{6,5},{7,6},{0,7},{9,8},{10,9},{11,1... | collective-permute-start | bytes 786440 | tf_op jit(solution)/shard_map/ppermute | solution.py:52
  10.3 0.1 fusion.38
  10.5 0.2 copy.31
  10.8 0.6 collective-permute-done
  11.5 5.7 %collective-permute-done.1 = bf16[2,128,512]{2,1,0:T(8,128)(2,1)S(1)} collective-permute-done((bf16[2,128,512]{2,1,0:T(8,128)(2,1)S(1)}, bf16[2,128,512]{2,1,0:T(8,128)(2,1)S(1)}, u32[]{:S(2)}, u32[]{:S(2)}) %collective-permute-start.1) | collective-permute-done | bytes 262176 | tf_op jit(solution)/shard_map/ppermute | solution.py:52
  17.2 4.9 %collective-permute-start.2 = (bf16[4,128,512]{2,1,0:T(8,128)(2,1)S(1)}, bf16[4,128,512]{2,1,0:T(8,128)(2,1)S(1)}, u32[]{:S(2)}, u32[]{:S(2)}) collective-permute-start(bf16[4,128,512]{2,1,0:T(8,128)(2,1)S(1)} %pad_maximum_fusion.2), channel_id=1, source_target_pairs={{8,0},{16,8},{24,16},{32,24},{40,32},{48,40},{56,48},{64,56},{72,6... | collective-permute-start | bytes 1572872 | tf_op jit(solution)/shard_map/ppermute | solution.py:52
  22.2 8.0 %collective-permute-done.2 = bf16[4,128,512]{2,1,0:T(8,128)(2,1)S(1)} collective-permute-done((bf16[4,128,512]{2,1,0:T(8,128)(2,1)S(1)}, bf16[4,128,512]{2,1,0:T(8,128)(2,1)S(1)}, u32[]{:S(2)}, u32[]{:S(2)}) %collective-permute-start.2) | collective-permute-done | bytes 524320 | tf_op jit(solution)/shard_map/ppermute | solution.py:52
  30.3 1.0 %fusion.15 = bf16[4,256,512]{2,1,0:T(8,128)(2,1)S(1)} fusion(bf16[1,640,512]{2,1,0:T(8,128)(2,1)S(1)} %bitcast.109, bf16[1,640,512]{2,1,0:T(8,128)(2,1)S(1)} %bitcast.107, bf16[1,640,512]{2,1,0:T(8,128)(2,1)S(1)} %bitcast.108, bf16[1,640,512]{2,1,0:T(8,128)(2,1)S(1)} %bitcast.110, f32[4,640]{1,0:T(4,128)S(1)} %bitcast.111, f32[256,640]{1,0:T(8,128)S(1)} %copy-done.1), kind=kOutput, calls=%fused_computation.16 | convolution fusion | flops 676855808 | bytes 4335616 | tf_op jit(solution)/shard_map/dot_general | solution.py:96
  31.5 0.2 copy.42
  31.7 0.2 copy.43
  31.9 0.5 maximum_bitcast_fusion
  32.5 1.3 %fusion.8 = f32[2,512,512]{1,2,0:T(8,128)S(1)} fusion(bf16[1,1024,512]{1,2,0:T(8,128)(2,1)S(1)} %get-tuple-element.9, bf16[1,1024,512]{1,2,0:T(8,128)(2,1)S(1)} %get-tuple-element.6, bf16[1,1024,512]{1,2,0:T(8,128)(2,1)S(1)} %get-tuple-element.10, bf16[1,1024,512]{1,2,0:T(8,128)(2,1)S(1)} %get-tuple-element.5), kind=kOutput, calls=%fused_computation.9 | convolution fusion | flops 1075838976 | bytes 6291456 | tf_op jit(solution)/shard_map/dot_general | solution.py:106
  33.8 0.2 copy.37
  34.0 30.6 %all_to_all.8 = f32[2,512,8,64]{1,3,0,2:T(8,128)S(1)} all-to-all(f32[2,512,8,64]{1,3,0,2:T(8,128)S(1)} %copy.37), channel_id=1, replica_groups=mesh['axial'=64,'circ'=8] {'circ'}, dimensions={2} | all-to-all | bytes 4194304 | tf_op jit(solution)/shard_map/all_to_all | solution.py:113
  64.6 0.2 reduce_sum.18
  64.8 0.2 copy.39
  65.0 0.3 reshape.59
  65.4 28.7 %all_to_all.9 = f32[64,1,1024]{2,1,0:T(1,128)S(1)} all-to-all(f32[64,1,1024]{2,1,0:T(1,128)S(1)} %reshape.59), channel_id=1, replica_groups=mesh['axial'=64,'circ'=8] {'axial'}, dimensions={0} | all-to-all | bytes 524288 | tf_op jit(solution)/shard_map/all_to_all | solution.py:117
  94.1 0.5 broadcast.48
  94.6 1.3 %reduce.6 = f32[64,1024]{1,0:T(8,128)S(1)} reduce(f32[64,1,1024]{2,1,0:T(1,128)S(1)} %all_to_all.9, f32[]{:T(128)} %broadcast.48), dimensions={1}, to_apply=%all_to_all.5.reduce_sub_computation | reduce | bytes 524292 | tf_op jit(solution)/shard_map/all_to_all | solution.py:117
  95.8 0.1 reshape.60
  96.0 0.7 bitcast_reduce_fusion
  (28 shorter events, 0.7 us)
Async XLA Ops:
  0.0 9.6 %copy-start = (s32[1,1,3,20]{3,1,2,0:T(1,128)S(1)}, s32[1,1,3,20]{3,1,2,0:T(1,128)}, u32[]{:S(2)}) copy-start(s32[1,1,3,20]{3,1,2,0:T(1,128)} %param.7) | copy-start | bytes 724
  1.4 10.0 %collective-permute-start = (bf16[2,128,512]{2,1,0:T(8,128)(2,1)S(1)}, bf16[2,128,512]{2,1,0:T(8,128)(2,1)S(1)}, u32[]{:S(2)}, u32[]{:S(2)}) collective-permute-start(bf16[2,128,512]{2,1,0:T(8,128)(2,1)S(1)} %get-tuple-element.22), channel_id=1, source_target_pairs={{7,0},{0,1},{1,2},{2,3},{3,4},{4,5},{5,6},{6,7},{15,8},{8,9},{9,10... | collective-permute-start | bytes 786440 | tf_op jit(solution)/shard_map/ppermute | solution.py:52
  5.5 11.7 %collective-permute-start.1 = (bf16[2,128,512]{2,1,0:T(8,128)(2,1)S(1)}, bf16[2,128,512]{2,1,0:T(8,128)(2,1)S(1)}, u32[]{:S(2)}, u32[]{:S(2)}) collective-permute-start(bf16[2,128,512]{2,1,0:T(8,128)(2,1)S(1)} %get-tuple-element.23), channel_id=1, source_target_pairs={{1,0},{2,1},{3,2},{4,3},{5,4},{6,5},{7,6},{0,7},{9,8},{10,9},{11,1... | collective-permute-start | bytes 786440 | tf_op jit(solution)/shard_map/ppermute | solution.py:52
  11.5 18.9 %copy-start.1 = (f32[256,640]{1,0:T(8,128)S(1)}, f32[256,640]{1,0:T(8,128)}, u32[]{:S(2)}) copy-start(f32[256,640]{1,0:T(8,128)} %constant.21) | copy-start | bytes 1966084
  17.2 13.0 %collective-permute-start.2 = (bf16[4,128,512]{2,1,0:T(8,128)(2,1)S(1)}, bf16[4,128,512]{2,1,0:T(8,128)(2,1)S(1)}, u32[]{:S(2)}, u32[]{:S(2)}) collective-permute-start(bf16[4,128,512]{2,1,0:T(8,128)(2,1)S(1)} %pad_maximum_fusion.2), channel_id=1, source_target_pairs={{8,0},{16,8},{24,16},{32,24},{40,32},{48,40},{56,48},{64,56},{72,6... | collective-permute-start | bytes 1572872 | tf_op jit(solution)/shard_map/ppermute | solution.py:52

commit v7 on v2

--- a/solution.py
+++ b/solution.py
@@ -119,10 +119,10 @@
         summand.reshape(2, mode_count, n_ci, cols), "circ", 2, 0, tiled=True
     )
     partial_value = parts.reshape(n_ci, 2, mode_count, cols).sum(axis=0)
-    parts = lax.all_to_all(
-        partial_value.reshape(2, n_ax, rows, cols), "axial", 1, 0, tiled=True
-    )
-    return parts.reshape(n_ax, 2, rows, cols).sum(axis=0)
+    arranged = partial_value.reshape(2, n_ax, rows, cols).transpose(1, 0, 2, 3)
+    arranged = arranged.reshape(n_ax, 2 * rows * cols // 128, 128)
+    parts = lax.all_to_all(arranged, "axial", 0, 0, tiled=True)
+    return parts.sum(axis=0).reshape(2, rows, cols)
 
 
 def solution(mesh):

time: 96 us -> 93.9 us (0.978)
  other arithmetic: 4.17 us -> 2.3 us
    all_to_all x1 -> x0, other arithmetic: 1.26 us -> none  [body(): lax.all_to_all(partial_value.reshape(2, n_ax, rows, cols), 'axial', 1, 0,...]
    unnamed x17 -> x14, local copies, waits for them, and re-layouts: 3.31 us -> 2.81 us
where the time goes in v7:
time: 93.9 us; the launch traced here: 93.4 us
  blocking collectives  60.7 us (65%)
  starting transfers between devices  19.9 us (21%)
  local copies, waits for them, and re-layouts  5.6 us (6%)
  matrix products  3.51 us (4%)
  other arithmetic  2.3 us (2%)
    all_to_all x1, blocking collectives, body(): lax.all_to_all(summand.reshape(2, mode_count, n_ci, cols), 'circ', 2, 0,...  35.3 us
    all_to_all x1, blocking collectives, body(): parts = lax.all_to_all(arranged, 'axial', 0, 0, tiled=True)  25.3 us
    ppermute x5, starting transfers between devices, shifted(): return lax.ppermute(block, axes if len(axes) > 1 else axes[0], pairs)  19.9 us
    unnamed x14, local copies, waits for them, and re-layouts  2.81 us
    dot_general x1, matrix products, body(): lax.dot_general(lhs, columns, (((2,), (1,)), ((0,), (0,))), preferred_ele...  2.1 us
  transfers between devices with their start and end apart: 5, of which 1 were waited for; matrix products, arithmetic and copies ran while one was open for 4% of the time, Pallas kernels for 0%

profile of v7, /device:TPU:1, one launch (start us, length us, event | category | flops | bytes accessed | tf_op | source)
XLA Modules:
  0.0 93.4 jit_solution(388215844775367977)
XLA Ops:
  0.0 1.4 %multiply_convert_fusion.2 = bf16[2,2,128,512]{3,2,1,0:T(8,128)(2,1)S(1)} fusion(f32[2,2,128,512]{3,2,1,0:T(8,128)} %param.5, f32[2,2,128]{2,1,0:T(2,128)} %param.6), kind=kLoop, calls=%fused_computation.25 | loop fusion | flops 524288 | bytes 1574912 | tf_op jit(solution)/shard_map/convert_element_type | solution.py:58
  1.4 4.0 %collective-permute-start = (bf16[128,512]{1,0:T(8,128)(2,1)S(1)}, bf16[128,512]{1,0:T(8,128)(2,1)S(1)}, u32[]{:S(2)}, u32[]{:S(2)}) collective-permute-start(bf16[128,512]{1,0:T(8,128)(2,1)S(1)} %get-tuple-element.18), channel_id=1, source_target_pairs={{7,0},{0,1},{1,2},{2,3},{3,4},{4,5},{5,6},{6,7},{15,8},{8,9},{9,10... | collective-permute-start | bytes 393224 | tf_op jit(solution)/shard_map/ppermute | solution.py:52
  5.5 4.1 %collective-permute-start.1 = (bf16[2,128,512]{2,1,0:T(8,128)(2,1)S(1)}, bf16[2,128,512]{2,1,0:T(8,128)(2,1)S(1)}, u32[]{:S(2)}, u32[]{:S(2)}) collective-permute-start(bf16[2,128,512]{2,1,0:T(8,128)(2,1)S(1)} %slice_bitcast_fusion.1), channel_id=1, source_target_pairs={{1,0},{2,1},{3,2},{4,3},{5,4},{6,5},{7,6},{0,7},{9,8},{10,9},{11,1... | collective-permute-start | bytes 786440 | tf_op jit(solution)/shard_map/ppermute | solution.py:52
  9.6 6.1 %collective-permute-start.2 = (bf16[128,512]{1,0:T(8,128)(2,1)S(1)}, bf16[128,512]{1,0:T(8,128)(2,1)S(1)}, u32[]{:S(2)}, u32[]{:S(2)}) collective-permute-start(bf16[128,512]{1,0:T(8,128)(2,1)S(1)} %get-tuple-element.19), channel_id=1, source_target_pairs={{15,0},{8,1},{9,2},{10,3},{11,4},{12,5},{13,6},{14,7},{23,8},{16,9... | collective-permute-start | bytes 393224 | tf_op jit(solution)/shard_map/ppermute | solution.py:52
  15.7 3.8 %collective-permute-start.3 = (bf16[2,128,512]{2,1,0:T(8,128)(2,1)S(1)}, bf16[2,128,512]{2,1,0:T(8,128)(2,1)S(1)}, u32[]{:S(2)}, u32[]{:S(2)}) collective-permute-start(bf16[2,128,512]{2,1,0:T(8,128)(2,1)S(1)} %slice_bitcast_fusion), channel_id=1, source_target_pairs={{8,0},{16,8},{24,16},{32,24},{40,32},{48,40},{56,48},{64,56},{72,6... | collective-permute-start | bytes 786440 | tf_op jit(solution)/shard_map/ppermute | solution.py:52
  19.5 1.9 %collective-permute-start.4 = (bf16[128,512]{1,0:T(8,128)(2,1)S(1)}, bf16[128,512]{1,0:T(8,128)(2,1)S(1)}, u32[]{:S(2)}, u32[]{:S(2)}) collective-permute-start(bf16[128,512]{1,0:T(8,128)(2,1)S(1)} %get-tuple-element.20), channel_id=1, source_target_pairs={{9,0},{10,1},{11,2},{12,3},{13,4},{14,5},{15,6},{8,7},{17,8},{18,9... | collective-permute-start | bytes 393224 | tf_op jit(solution)/shard_map/ppermute | solution.py:52
  21.4 0.7 constant_dynamic-update-slice_fusion.3
  22.9 0.2 copy.29
  23.3 0.7 constant_dynamic-update-slice_fusion.2
  24.0 0.7 constant_dynamic-update-slice_fusion.1
  24.6 0.7 fusion.31
  25.3 0.7 constant_dynamic-update-slice_fusion
  26.1 0.5 collective-permute-done.4
  26.7 2.1 %fusion.15 = bf16[4,256,512]{2,1,0:T(8,128)(2,1)S(1)} fusion(bf16[1,640,512]{2,1,0:T(8,128)(2,1)S(1)} %bitcast.97, bf16[1,640,512]{2,1,0:T(8,128)(2,1)S(1)} %bitcast.98, bf16[1,640,512]{2,1,0:T(8,128)(2,1)S(1)} %bitcast.99, bf16[1,640,512]{2,1,0:T(8,128)(2,1)} %bitcast.100, f32[4,640]{1,0:T(4,128)S(1)} %bitcast.101, f32[256,640]{1,0:T(8,128)S(1)} %copy-done.1), kind=kOutput, calls=%fused_computation.16 | convolution fusion | flops 676855808 | bytes 4335616 | tf_op jit(solution)/shard_map/dot_general | solution.py:101
  28.9 0.2 copy.40
  29.1 0.2 copy.41
  29.4 0.5 maximum_bitcast_fusion
  29.9 1.3 %fusion.8 = f32[2,512,512]{1,2,0:T(8,128)S(1)} fusion(bf16[1,1024,512]{1,2,0:T(8,128)(2,1)S(1)} %get-tuple-element.9, bf16[1,1024,512]{1,2,0:T(8,128)(2,1)S(1)} %get-tuple-element.6, bf16[1,1024,512]{1,2,0:T(8,128)(2,1)S(1)} %get-tuple-element.10, bf16[1,1024,512]{1,2,0:T(8,128)(2,1)S(1)} %get-tuple-element.5), kind=kOutput, calls=%fused_computation.9 | convolution fusion | flops 1075838976 | bytes 6291456 | tf_op jit(solution)/shard_map/dot_general | solution.py:111
  31.2 0.2 copy.35
  31.4 35.3 %all_to_all.14 = f32[2,512,8,64]{1,3,0,2:T(8,128)S(1)} all-to-all(f32[2,512,8,64]{1,3,0,2:T(8,128)S(1)} %copy.35), channel_id=1, replica_groups=mesh['axial'=64,'circ'=8] {'circ'}, dimensions={2} | all-to-all | bytes 4194304 | tf_op jit(solution)/shard_map/all_to_all | solution.py:118
  66.8 0.2 reduce_sum.18
  67.0 0.2 copy.37
  67.4 25.3 %all_to_all.15 = f32[64,8,128]{2,1,0:T(8,128)S(1)} all-to-all(f32[64,8,128]{2,1,0:T(8,128)S(1)} %reshape.63), channel_id=1, replica_groups=mesh['axial'=64,'circ'=8] {'axial'}, dimensions={0} | all-to-all | bytes 524288 | tf_op jit(solution)/shard_map/all_to_all | solution.py:124
  92.8 0.7 reshape.64
  (28 shorter events, 0.8 us)
Async XLA Ops:
  0.0 22.1 %copy-start = (s32[1,1,3,20]{3,1,2,0:T(1,128)S(1)}, s32[1,1,3,20]{3,1,2,0:T(1,128)}, u32[]{:S(2)}) copy-start(s32[1,1,3,20]{3,1,2,0:T(1,128)} %param.7) | copy-start | bytes 724
  1.4 22.5 %collective-permute-start = (bf16[128,512]{1,0:T(8,128)(2,1)S(1)}, bf16[128,512]{1,0:T(8,128)(2,1)S(1)}, u32[]{:S(2)}, u32[]{:S(2)}) collective-permute-start(bf16[128,512]{1,0:T(8,128)(2,1)S(1)} %get-tuple-element.18), channel_id=1, source_target_pairs={{7,0},{0,1},{1,2},{2,3},{3,4},{4,5},{5,6},{6,7},{15,8},{8,9},{9,10... | collective-permute-start | bytes 393224 | tf_op jit(solution)/shard_map/ppermute | solution.py:52
  5.5 19.8 %collective-permute-start.1 = (bf16[2,128,512]{2,1,0:T(8,128)(2,1)S(1)}, bf16[2,128,512]{2,1,0:T(8,128)(2,1)S(1)}, u32[]{:S(2)}, u32[]{:S(2)}) collective-permute-start(bf16[2,128,512]{2,1,0:T(8,128)(2,1)S(1)} %slice_bitcast_fusion.1), channel_id=1, source_target_pairs={{1,0},{2,1},{3,2},{4,3},{5,4},{6,5},{7,6},{0,7},{9,8},{10,9},{11,1... | collective-permute-start | bytes 786440 | tf_op jit(solution)/shard_map/ppermute | solution.py:52
  9.6 16.4 %collective-permute-start.2 = (bf16[128,512]{1,0:T(8,128)(2,1)S(1)}, bf16[128,512]{1,0:T(8,128)(2,1)S(1)}, u32[]{:S(2)}, u32[]{:S(2)}) collective-permute-start(bf16[128,512]{1,0:T(8,128)(2,1)S(1)} %get-tuple-element.19), channel_id=1, source_target_pairs={{15,0},{8,1},{9,2},{10,3},{11,4},{12,5},{13,6},{14,7},{23,8},{16,9... | collective-permute-start | bytes 393224 | tf_op jit(solution)/shard_map/ppermute | solution.py:52
  15.7 10.4 %collective-permute-start.3 = (bf16[2,128,512]{2,1,0:T(8,128)(2,1)S(1)}, bf16[2,128,512]{2,1,0:T(8,128)(2,1)S(1)}, u32[]{:S(2)}, u32[]{:S(2)}) collective-permute-start(bf16[2,128,512]{2,1,0:T(8,128)(2,1)S(1)} %slice_bitcast_fusion), channel_id=1, source_target_pairs={{8,0},{16,8},{24,16},{32,24},{40,32},{48,40},{56,48},{64,56},{72,6... | collective-permute-start | bytes 786440 | tf_op jit(solution)/shard_map/ppermute | solution.py:52
  19.5 7.2 %collective-permute-start.4 = (bf16[128,512]{1,0:T(8,128)(2,1)S(1)}, bf16[128,512]{1,0:T(8,128)(2,1)S(1)}, u32[]{:S(2)}, u32[]{:S(2)}) collective-permute-start(bf16[128,512]{1,0:T(8,128)(2,1)S(1)} %get-tuple-element.20), channel_id=1, source_target_pairs={{9,0},{10,1},{11,2},{12,3},{13,4},{14,5},{15,6},{8,7},{17,8},{18,9... | collective-permute-start | bytes 393224 | tf_op jit(solution)/shard_map/ppermute | solution.py:52
  23.3 3.4 %copy-start.1 = (f32[256,640]{1,0:T(8,128)S(1)}, f32[256,640]{1,0:T(8,128)}, u32[]{:S(2)}) copy-start(f32[256,640]{1,0:T(8,128)} %constant.21) | copy-start | bytes 1966084

commit v8 on v3

--- a/solution.py
+++ b/solution.py
@@ -124,11 +124,16 @@
     n_ci = group_size(CIRC)
     cols = mode_count // n_ci
     rows = mode_count // (outer * n_core)
-    arranged = summand.reshape(2, outer, n_core, rows, n_ci, cols).transpose(4, 2, 1, 0, 3, 5)
-    arranged = arranged.reshape(n_ci * n_core, outer * 2 * rows * cols)
-    parts = lax.all_to_all(arranged, CIRC + ("core",), 0, 0, tiled=True)
-    partial_value = parts.reshape(n_ci * n_core, outer, 2 * rows * cols).sum(axis=0)
-    parts = lax.all_to_all(partial_value, AXIAL[:-1], 0, 0, tiled=True)
+    split = summand.reshape(2, outer, n_core, rows, mode_count)
+    mine = lax.axis_index("core")
+    keep = lax.dynamic_index_in_dim(split, mine, axis=2, keepdims=False)
+    send = lax.dynamic_index_in_dim(split, n_core - 1 - mine, axis=2, keepdims=False)
+    pairs = [(k, n_core - 1 - k) for k in range(n_core)]
+    half = keep + lax.ppermute(send, "core", pairs)
+    parts = lax.all_to_all(half.reshape(2, outer, rows, n_ci, cols), CIRC, 3, 0, tiled=True)
+    partial_value = parts.reshape(n_ci, 2, outer, rows, cols).sum(axis=0)
+    arranged = partial_value.transpose(1, 0, 2, 3).reshape(outer, 2 * rows * cols // 128, 128)
+    parts = lax.all_to_all(arranged, AXIAL[:-1], 0, 0, tiled=True)
     return parts.sum(axis=0).reshape(2, rows, cols)
 
 

time: 105 us -> 102 us (0.971)
  blocking collectives: 59.8 us -> 48.9 us
  other arithmetic: 4.94 us -> 9.01 us
  starting transfers between devices: 18.9 us -> 21.8 us
  waiting for transfers between devices: 4.28 us -> 6.96 us
  local copies, waits for them, and re-layouts: 13 us -> 10.8 us
    all_to_all x2, blocking collectives: 59.8 us -> 48.9 us  [the longest x1 24.9 us: body(): parts = lax.all_to_all(arranged, AXIAL[:-1], 0, 0, tiled=True)]
    unnamed x14 -> x16, local copies, waits for them, and re-layouts: 0.2 us -> 4.81 us
    all_to_all x0 -> x1, other arithmetic: none -> 4.5 us  [body(): lax.all_to_all(half.reshape(2, outer, rows, n_ci, cols), CIRC, 3, 0, tile...]
    all_to_all x1, local copies, waits for them, and re-layouts: 4.52 us -> 0.51 us  [body(): lax.all_to_all(half.reshape(2, outer, rows, n_ci, cols), CIRC, 3, 0, tile...]
    reshape x2 -> x3, local copies, waits for them, and re-layouts: 7.36 us -> 3.39 us  [the longest x2 3.3 us: body(): half.reshape(2, outer, rows, n_ci, cols)]
    ppermute x0 -> x1, waiting for transfers between devices: none -> 2.97 us  [body(): half = keep + lax.ppermute(send, 'core', pairs)]
    reduce_sum x1, other arithmetic: 2.95 us -> 0.16 us  [body(): partial_value = parts.reshape(n_ci, 2, outer, rows, cols).sum(axis=0)]
    add x0 -> x1, other arithmetic: none -> 2.46 us  [body(): half = keep + lax.ppermute(send, 'core', pairs)]
  transfers between devices with their start and end apart: 5 -> 6, of which waited for: 2 -> 3; matrix products, arithmetic and copies ran while one was open for 0% -> 1% of each run, Pallas kernels for 0% -> 0%
where the time goes in v8:
time: 102 us; the launch traced here: 101 us
  blocking collectives  48.9 us (48%)
  starting transfers between devices  21.8 us (21%)
  local copies, waits for them, and re-layouts  10.8 us (11%)
  other arithmetic  9.01 us (9%)
  waiting for transfers between devices  6.96 us (7%)
  matrix products  2.42 us (2%)
    all_to_all x1, blocking collectives, body(): parts = lax.all_to_all(arranged, AXIAL[:-1], 0, 0, tiled=True)  24.9 us
    all_to_all x1, blocking collectives, body(): lax.all_to_all(half.reshape(2, outer, rows, n_ci, cols), CIRC, 3, 0, tile...  24 us
    ppermute x5, starting transfers between devices, shifted(): return lax.ppermute(block, sum(axes, ()), pairs)  19.9 us
    unnamed x16, local copies, waits for them, and re-layouts  4.81 us
    all_to_all x1, other arithmetic, body(): lax.all_to_all(half.reshape(2, outer, rows, n_ci, cols), CIRC, 3, 0, tile...  4.5 us
    ppermute x5, waiting for transfers between devices, shifted(): return lax.ppermute(block, sum(axes, ()), pairs)  4 us
    reshape x2, local copies, waits for them, and re-layouts, body(): half.reshape(2, outer, rows, n_ci, cols)  3.3 us
    ppermute x1, waiting for transfers between devices, body(): half = keep + lax.ppermute(send, 'core', pairs)  2.97 us
  transfers between devices with their start and end apart: 6, of which 3 were waited for; matrix products, arithmetic and copies ran while one was open for 1% of the time, Pallas kernels for 0%

profile of v8, /device:TPU:1, one launch (start us, length us, event | category | flops | bytes accessed | tf_op | source)
XLA Modules:
  0.0 100.8 jit_solution(175937155847803109)
XLA Ops:
  0.0 1.4 %multiply_convert_fusion.2 = bf16[2,2,128,512]{3,2,1,0:T(8,128)(2,1)S(1)} fusion(f32[2,2,128,512]{3,2,1,0:T(8,128)} %param.5, f32[2,2,128]{2,1,0:T(2,128)} %param.6), kind=kLoop, calls=%fused_computation.27 | loop fusion | flops 524288 | bytes 1574912 | tf_op jit(solution)/shard_map/convert_element_type | solution.py:66
  1.4 4.0 %collective-permute-start = (bf16[128,512]{1,0:T(8,128)(2,1)S(1)}, bf16[128,512]{1,0:T(8,128)(2,1)S(1)}, u32[]{:S(2)}, u32[]{:S(2)}) collective-permute-start(bf16[128,512]{1,0:T(8,128)(2,1)S(1)} %get-tuple-element.18), channel_id=1, source_target_pairs={{7,0},{0,1},{1,2},{2,3},{3,4},{4,5},{5,6},{6,7},{15,8},{8,9},{9,10... | collective-permute-start | bytes 393224 | tf_op jit(solution)/shard_map/ppermute | solution.py:60
  5.5 4.1 %collective-permute-start.1 = (bf16[2,128,512]{2,1,0:T(8,128)(2,1)S(1)}, bf16[2,128,512]{2,1,0:T(8,128)(2,1)S(1)}, u32[]{:S(2)}, u32[]{:S(2)}) collective-permute-start(bf16[2,128,512]{2,1,0:T(8,128)(2,1)S(1)} %slice_bitcast_fusion.1), channel_id=1, source_target_pairs={{1,0},{2,1},{3,2},{4,3},{5,4},{6,5},{7,6},{0,7},{9,8},{10,9},{11,1... | collective-permute-start | bytes 786440 | tf_op jit(solution)/shard_map/ppermute | solution.py:60
  9.6 6.1 %collective-permute-start.2 = (bf16[128,512]{1,0:T(8,128)(2,1)S(1)}, bf16[128,512]{1,0:T(8,128)(2,1)S(1)}, u32[]{:S(2)}, u32[]{:S(2)}) collective-permute-start(bf16[128,512]{1,0:T(8,128)(2,1)S(1)} %get-tuple-element.19), channel_id=1, source_target_pairs={{15,0},{8,1},{9,2},{10,3},{11,4},{12,5},{13,6},{14,7},{23,8},{16,9... | collective-permute-start | bytes 393224 | tf_op jit(solution)/shard_map/ppermute | solution.py:60
  15.7 3.8 %collective-permute-start.3 = (bf16[2,128,512]{2,1,0:T(8,128)(2,1)S(1)}, bf16[2,128,512]{2,1,0:T(8,128)(2,1)S(1)}, u32[]{:S(2)}, u32[]{:S(2)}) collective-permute-start(bf16[2,128,512]{2,1,0:T(8,128)(2,1)S(1)} %slice_bitcast_fusion), channel_id=1, source_target_pairs={{8,0},{16,8},{24,16},{32,24},{40,32},{48,40},{56,48},{64,56},{72,6... | collective-permute-start | bytes 786440 | tf_op jit(solution)/shard_map/ppermute | solution.py:60
  19.5 1.9 %collective-permute-start.4 = (bf16[128,512]{1,0:T(8,128)(2,1)S(1)}, bf16[128,512]{1,0:T(8,128)(2,1)S(1)}, u32[]{:S(2)}, u32[]{:S(2)}) collective-permute-start(bf16[128,512]{1,0:T(8,128)(2,1)S(1)} %get-tuple-element.20), channel_id=1, source_target_pairs={{9,0},{10,1},{11,2},{12,3},{13,4},{14,5},{15,6},{8,7},{17,8},{18,9... | collective-permute-start | bytes 393224 | tf_op jit(solution)/shard_map/ppermute | solution.py:60
  22.6 1.0 %collective-permute-done.3 = bf16[2,128,512]{2,1,0:T(8,128)(2,1)S(1)} collective-permute-done((bf16[2,128,512]{2,1,0:T(8,128)(2,1)S(1)}, bf16[2,128,512]{2,1,0:T(8,128)(2,1)S(1)}, u32[]{:S(2)}, u32[]{:S(2)}) %collective-permute-start.3) | collective-permute-done | bytes 262176 | tf_op jit(solution)/shard_map/ppermute | solution.py:60
  23.7 2.9 %collective-permute-done.4 = bf16[128,512]{1,0:T(8,128)(2,1)S(1)} collective-permute-done((bf16[128,512]{1,0:T(8,128)(2,1)S(1)}, bf16[128,512]{1,0:T(8,128)(2,1)S(1)}, u32[]{:S(2)}, u32[]{:S(2)}) %collective-permute-start.4) | collective-permute-done | bytes 131104 | tf_op jit(solution)/shard_map/ppermute | solution.py:60
  26.7 1.0 fusion.15
  27.8 0.4 maximum_bitcast_fusion
  28.2 1.3 %fusion.8 = f32[2,512,512]{2,1,0:T(8,128)S(1)} fusion(bf16[1,1024,512]{2,1,0:T(8,128)(2,1)S(1)} %get-tuple-element.9, bf16[1,1024,512]{2,1,0:T(8,128)(2,1)S(1)} %get-tuple-element.6, bf16[1,1024,512]{2,1,0:T(8,128)(2,1)S(1)} %get-tuple-element.10, bf16[1,1024,512]{2,1,0:T(8,128)(2,1)S(1)} %get-tuple-element.5), kind=kOutput, calls=%fused_computation.9 | convolution fusion | flops 1075838976 | bytes 6291456 | tf_op jit(solution)/shard_map/dot_general | solution.py:119
  29.5 1.1 %dynamic-slice_bitcast_fusion = f32[2,32,8,512]{3,2,1,0:T(8,128)} fusion(f32[2,32,2,8,512]{4,3,2,1,0:T(8,128)S(1)} %bitcast.103, s32[]{:T(128)S(6)} %select_n.17), kind=kLoop, calls=%fused_computation.26 | loop fusion | bytes 2097156 | tf_op jit(solution)/shard_map/jit(dynamic_index_in_dim)/squeeze | solution.py:130
  30.6 1.9 %collective-permute-start.5 = (f32[2,32,8,512]{3,2,1,0:T(8,128)}, f32[2,32,8,512]{3,2,1,0:T(8,128)}, u32[]{:S(2)}, u32[]{:S(2)}) collective-permute-start(f32[2,32,8,512]{3,2,1,0:T(8,128)} %dynamic-slice_bitcast_fusion), channel_id=1, source_target_pairs={{0,8},{8,0},{1,9},{9,1},{2,10},{10,2},{3,11},{11,3},{4,12},{12,4},... | collective-permute-start | bytes 3145736 | tf_op jit(solution)/shard_map/ppermute | solution.py:132
  32.6 3.0 %collective-permute-done.5 = f32[2,32,8,512]{3,2,1,0:T(8,128)} collective-permute-done((f32[2,32,8,512]{3,2,1,0:T(8,128)}, f32[2,32,8,512]{3,2,1,0:T(8,128)}, u32[]{:S(2)}, u32[]{:S(2)}) %collective-permute-start.5) | collective-permute-done | bytes 1048608 | tf_op jit(solution)/shard_map/ppermute | solution.py:132
  35.5 2.5 %bitcast_add_fusion = f32[2,32,8,512]{3,2,1,0:T(8,128)} fusion(f32[2,32,8,512]{3,2,1,0:T(8,128)} %collective-permute-done.5, f32[2,32,2,8,512]{4,3,2,1,0:T(8,128)S(1)} %bitcast.104, s32[]{:T(128)S(6)} %select_n.16), kind=kLoop, calls=%fused_computation.25 | loop fusion | flops 262144 | bytes 3145732 | tf_op jit(solution)/shard_map/add | solution.py:132
  38.0 1.6 %reshape.62 = f32[2,32,8,8,64]{4,3,2,1,0:T(8,128)S(1)} reshape(f32[2,32,8,512]{3,2,1,0:T(8,128)} %bitcast_add_fusion) | data formatting | bytes 2097152 | tf_op jit(solution)/shard_map/reshape | solution.py:133
  39.6 1.7 %copy.21 = f32[2,32,8,8,64]{4,2,1,0,3:T(8,128)} copy(f32[2,32,8,8,64]{4,3,2,1,0:T(8,128)S(1)} %reshape.62) | data formatting | bytes 2097152 | tf_op jit(solution)/shard_map/reshape | solution.py:133
  41.3 2.6 %reshape.65 = f32[8,1,32768]{2,1,0:T(1,128)S(1)} reshape(f32[8,2,32,8,64]{4,3,2,1,0:T(8,128)} %bitcast.102) | data formatting | bytes 2097152
  43.9 24.0 %all_to_all.14 = f32[8,1,32768]{2,1,0:T(1,128)S(1)} all-to-all(f32[8,1,32768]{2,1,0:T(1,128)S(1)} %reshape.65), channel_id=1, replica_groups=mesh['y_hi'=4,'z'=8,'core'=2,'x'=4,'y_lo'=2] {'x','y_lo'}, dimensions={0} | all-to-all | bytes 2097152 | tf_op jit(solution)/shard_map/all_to_all | solution.py:133
  67.9 0.5 broadcast.48
  68.4 4.5 %reduce.3 = f32[8,32768]{1,0:T(8,128)} reduce(f32[8,1,32768]{2,1,0:T(1,128)S(1)} %all_to_all.14, f32[]{:T(128)} %broadcast.48), dimensions={1}, to_apply=%all_to_all.4.reduce_sub_computation | reduce | bytes 2097156 | tf_op jit(solution)/shard_map/all_to_all | solution.py:133
  72.9 2.1 %reshape.66 = f32[8,2,32,8,64]{4,3,2,1,0:T(8,128)S(1)} reshape(f32[8,32768]{1,0:T(8,128)} %reduce.3) | data formatting | bytes 2097152
  75.3 24.9 %all_to_all.15 = f32[32,8,128]{2,1,0:T(8,128)S(1)} all-to-all(f32[32,8,128]{2,1,0:T(8,128)S(1)} %reshape.63), channel_id=1, replica_groups=mesh['y_hi'=4,'z'=8,'core'=2,'x'=4,'y_lo'=2] {'y_hi','z'}, dimensions={0} | all-to-all | bytes 262144 | tf_op jit(solution)/shard_map/all_to_all | solution.py:136
  100.2 0.7 reshape.64
  (33 shorter events, 0.9 us)
Async XLA Ops:
  0.0 21.5 %copy-start = (s32[1,1,3,20]{3,1,2,0:T(1,128)S(1)}, s32[1,1,3,20]{3,1,2,0:T(1,128)}, u32[]{:S(2)}) copy-start(s32[1,1,3,20]{3,1,2,0:T(1,128)} %param.7) | copy-start | bytes 724
  1.4 21.0 %collective-permute-start = (bf16[128,512]{1,0:T(8,128)(2,1)S(1)}, bf16[128,512]{1,0:T(8,128)(2,1)S(1)}, u32[]{:S(2)}, u32[]{:S(2)}) collective-permute-start(bf16[128,512]{1,0:T(8,128)(2,1)S(1)} %get-tuple-element.18), channel_id=1, source_target_pairs={{7,0},{0,1},{1,2},{2,3},{3,4},{4,5},{5,6},{6,7},{15,8},{8,9},{9,10... | collective-permute-start | bytes 393224 | tf_op jit(solution)/shard_map/ppermute | solution.py:60
  5.5 17.0 %collective-permute-start.1 = (bf16[2,128,512]{2,1,0:T(8,128)(2,1)S(1)}, bf16[2,128,512]{2,1,0:T(8,128)(2,1)S(1)}, u32[]{:S(2)}, u32[]{:S(2)}) collective-permute-start(bf16[2,128,512]{2,1,0:T(8,128)(2,1)S(1)} %slice_bitcast_fusion.1), channel_id=1, source_target_pairs={{1,0},{2,1},{3,2},{4,3},{5,4},{6,5},{7,6},{0,7},{9,8},{10,9},{11,1... | collective-permute-start | bytes 786440 | tf_op jit(solution)/shard_map/ppermute | solution.py:60
  9.6 13.0 %collective-permute-start.2 = (bf16[128,512]{1,0:T(8,128)(2,1)S(1)}, bf16[128,512]{1,0:T(8,128)(2,1)S(1)}, u32[]{:S(2)}, u32[]{:S(2)}) collective-permute-start(bf16[128,512]{1,0:T(8,128)(2,1)S(1)} %get-tuple-element.19), channel_id=1, source_target_pairs={{15,0},{8,1},{9,2},{10,3},{11,4},{12,5},{13,6},{14,7},{23,8},{16,9... | collective-permute-start | bytes 393224 | tf_op jit(solution)/shard_map/ppermute | solution.py:60
  15.7 8.0 %collective-permute-start.3 = (bf16[2,128,512]{2,1,0:T(8,128)(2,1)S(1)}, bf16[2,128,512]{2,1,0:T(8,128)(2,1)S(1)}, u32[]{:S(2)}, u32[]{:S(2)}) collective-permute-start(bf16[2,128,512]{2,1,0:T(8,128)(2,1)S(1)} %slice_bitcast_fusion), channel_id=1, source_target_pairs={{8,0},{16,8},{24,16},{32,24},{40,32},{48,40},{56,48},{64,56},{72,6... | collective-permute-start | bytes 786440 | tf_op jit(solution)/shard_map/ppermute | solution.py:60
  19.5 7.2 %collective-permute-start.4 = (bf16[128,512]{1,0:T(8,128)(2,1)S(1)}, bf16[128,512]{1,0:T(8,128)(2,1)S(1)}, u32[]{:S(2)}, u32[]{:S(2)}) collective-permute-start(bf16[128,512]{1,0:T(8,128)(2,1)S(1)} %get-tuple-element.20), channel_id=1, source_target_pairs={{9,0},{10,1},{11,2},{12,3},{13,4},{14,5},{15,6},{8,7},{17,8},{18,9... | collective-permute-start | bytes 393224 | tf_op jit(solution)/shard_map/ppermute | solution.py:60
  22.4 4.3 %copy-start.1 = (f32[256,640]{1,0:T(8,128)S(1)}, f32[256,640]{1,0:T(8,128)}, u32[]{:S(2)}) copy-start(f32[256,640]{1,0:T(8,128)} %constant.37) | copy-start | bytes 1966084
  30.6 4.9 %collective-permute-start.5 = (f32[2,32,8,512]{3,2,1,0:T(8,128)}, f32[2,32,8,512]{3,2,1,0:T(8,128)}, u32[]{:S(2)}, u32[]{:S(2)}) collective-permute-start(f32[2,32,8,512]{3,2,1,0:T(8,128)} %dynamic-slice_bitcast_fusion), channel_id=1, source_target_pairs={{0,8},{8,0},{1,9},{9,1},{2,10},{10,2},{3,11},{11,3},{4,12},{12,4},... | collective-permute-start | bytes 3145736 | tf_op jit(solution)/shard_map/ppermute | solution.py:132

commit v9 on v8

--- a/solution.py
+++ b/solution.py
@@ -130,8 +130,10 @@
     send = lax.dynamic_index_in_dim(split, n_core - 1 - mine, axis=2, keepdims=False)
     pairs = [(k, n_core - 1 - k) for k in range(n_core)]
     half = keep + lax.ppermute(send, "core", pairs)
-    parts = lax.all_to_all(half.reshape(2, outer, rows, n_ci, cols), CIRC, 3, 0, tiled=True)
-    partial_value = parts.reshape(n_ci, 2, outer, rows, cols).sum(axis=0)
+    arranged = half.reshape(2, outer, rows, n_ci, cols).transpose(3, 0, 1, 2, 4)
+    arranged = arranged.reshape(n_ci, 2 * outer * rows * cols // 128, 128)
+    parts = lax.all_to_all(arranged, CIRC, 0, 0, tiled=True)
+    partial_value = parts.sum(axis=0).reshape(2, outer, rows, cols)
     arranged = partial_value.transpose(1, 0, 2, 3).reshape(outer, 2 * rows * cols // 128, 128)
     parts = lax.all_to_all(arranged, AXIAL[:-1], 0, 0, tiled=True)
     return parts.sum(axis=0).reshape(2, rows, cols)

time: 102 us -> 93.9 us (0.921)
  other arithmetic: 9.01 us -> 4.37 us
  local copies, waits for them, and re-layouts: 10.8 us -> 7.5 us
    unnamed x16 -> x14, local copies, waits for them, and re-layouts: 4.81 us -> 0.2 us
    all_to_all x1 -> x0, other arithmetic: 4.5 us -> none  [body(): lax.all_to_all(half.reshape(2, outer, rows, n_ci, cols), CIRC, 3, 0, tile...]
    transpose x0 -> x1, local copies, waits for them, and re-layouts: none -> 1.71 us  [body(): arranged = half.reshape(2, outer, rows, n_ci, cols).transpose(3, 0, 1, 2, 4)]
    reshape x2 -> x3, local copies, waits for them, and re-layouts: 3.3 us -> 3.48 us  [the longest x1 1.8 us: body(): arranged = arranged.reshape(n_ci, 2 * outer * rows * cols // 128, 128)]
where the time goes in v9:
time: 93.9 us; the launch traced here: 92.9 us
  blocking collectives  48.9 us (52%)
  starting transfers between devices  21.8 us (23%)
  local copies, waits for them, and re-layouts  7.5 us (8%)
  waiting for transfers between devices  6.96 us (7%)
  other arithmetic  4.37 us (5%)
  matrix products  2.42 us (3%)
  between operations  0.96 us (1%)
    all_to_all x1, blocking collectives, body(): parts = lax.all_to_all(arranged, AXIAL[:-1], 0, 0, tiled=True)  24.9 us
    all_to_all x1, blocking collectives, body(): parts = lax.all_to_all(arranged, CIRC, 0, 0, tiled=True)  24 us
    ppermute x5, starting transfers between devices, shifted(): return lax.ppermute(block, sum(axes, ()), pairs)  19.9 us
    ppermute x5, waiting for transfers between devices, shifted(): return lax.ppermute(block, sum(axes, ()), pairs)  4 us
    ppermute x1, waiting for transfers between devices, body(): half = keep + lax.ppermute(send, 'core', pairs)  2.97 us
    add x1, other arithmetic, body(): half = keep + lax.ppermute(send, 'core', pairs)  2.43 us
    ppermute x1, starting transfers between devices, body(): half = keep + lax.ppermute(send, 'core', pairs)  1.91 us
  transfers between devices with their start and end apart: 6, of which 3 were waited for; matrix products, arithmetic and copies ran while one was open for 1% of the time, Pallas kernels for 0%

profile of v9, /device:TPU:1, one launch (start us, length us, event | category | flops | bytes accessed | tf_op | source)
XLA Modules:
  0.0 92.9 jit_solution(295512512565761428)
XLA Ops:
  0.0 1.4 %multiply_convert_fusion.2 = bf16[2,2,128,512]{3,2,1,0:T(8,128)(2,1)S(1)} fusion(f32[2,2,128,512]{3,2,1,0:T(8,128)} %param.5, f32[2,2,128]{2,1,0:T(2,128)} %param.6), kind=kLoop, calls=%fused_computation.27 | loop fusion | flops 524288 | bytes 1574912 | tf_op jit(solution)/shard_map/convert_element_type | solution.py:66
  1.4 4.0 %collective-permute-start = (bf16[128,512]{1,0:T(8,128)(2,1)S(1)}, bf16[128,512]{1,0:T(8,128)(2,1)S(1)}, u32[]{:S(2)}, u32[]{:S(2)}) collective-permute-start(bf16[128,512]{1,0:T(8,128)(2,1)S(1)} %get-tuple-element.18), channel_id=1, source_target_pairs={{7,0},{0,1},{1,2},{2,3},{3,4},{4,5},{5,6},{6,7},{15,8},{8,9},{9,10... | collective-permute-start | bytes 393224 | tf_op jit(solution)/shard_map/ppermute | solution.py:60
  5.5 4.1 %collective-permute-start.1 = (bf16[2,128,512]{2,1,0:T(8,128)(2,1)S(1)}, bf16[2,128,512]{2,1,0:T(8,128)(2,1)S(1)}, u32[]{:S(2)}, u32[]{:S(2)}) collective-permute-start(bf16[2,128,512]{2,1,0:T(8,128)(2,1)S(1)} %slice_bitcast_fusion.1), channel_id=1, source_target_pairs={{1,0},{2,1},{3,2},{4,3},{5,4},{6,5},{7,6},{0,7},{9,8},{10,9},{11,1... | collective-permute-start | bytes 786440 | tf_op jit(solution)/shard_map/ppermute | solution.py:60
  9.6 6.1 %collective-permute-start.2 = (bf16[128,512]{1,0:T(8,128)(2,1)S(1)}, bf16[128,512]{1,0:T(8,128)(2,1)S(1)}, u32[]{:S(2)}, u32[]{:S(2)}) collective-permute-start(bf16[128,512]{1,0:T(8,128)(2,1)S(1)} %get-tuple-element.19), channel_id=1, source_target_pairs={{15,0},{8,1},{9,2},{10,3},{11,4},{12,5},{13,6},{14,7},{23,8},{16,9... | collective-permute-start | bytes 393224 | tf_op jit(solution)/shard_map/ppermute | solution.py:60
  15.7 3.8 %collective-permute-start.3 = (bf16[2,128,512]{2,1,0:T(8,128)(2,1)S(1)}, bf16[2,128,512]{2,1,0:T(8,128)(2,1)S(1)}, u32[]{:S(2)}, u32[]{:S(2)}) collective-permute-start(bf16[2,128,512]{2,1,0:T(8,128)(2,1)S(1)} %slice_bitcast_fusion), channel_id=1, source_target_pairs={{8,0},{16,8},{24,16},{32,24},{40,32},{48,40},{56,48},{64,56},{72,6... | collective-permute-start | bytes 786440 | tf_op jit(solution)/shard_map/ppermute | solution.py:60
  19.5 1.9 %collective-permute-start.4 = (bf16[128,512]{1,0:T(8,128)(2,1)S(1)}, bf16[128,512]{1,0:T(8,128)(2,1)S(1)}, u32[]{:S(2)}, u32[]{:S(2)}) collective-permute-start(bf16[128,512]{1,0:T(8,128)(2,1)S(1)} %get-tuple-element.20), channel_id=1, source_target_pairs={{9,0},{10,1},{11,2},{12,3},{13,4},{14,5},{15,6},{8,7},{17,8},{18,9... | collective-permute-start | bytes 393224 | tf_op jit(solution)/shard_map/ppermute | solution.py:60
  22.2 0.1 fusion.32
  22.6 1.0 %collective-permute-done.3 = bf16[2,128,512]{2,1,0:T(8,128)(2,1)S(1)} collective-permute-done((bf16[2,128,512]{2,1,0:T(8,128)(2,1)S(1)}, bf16[2,128,512]{2,1,0:T(8,128)(2,1)S(1)}, u32[]{:S(2)}, u32[]{:S(2)}) %collective-permute-start.3) | collective-permute-done | bytes 262176 | tf_op jit(solution)/shard_map/ppermute | solution.py:60
  23.7 2.9 %collective-permute-done.4 = bf16[128,512]{1,0:T(8,128)(2,1)S(1)} collective-permute-done((bf16[128,512]{1,0:T(8,128)(2,1)S(1)}, bf16[128,512]{1,0:T(8,128)(2,1)S(1)}, u32[]{:S(2)}, u32[]{:S(2)}) %collective-permute-start.4) | collective-permute-done | bytes 131104 | tf_op jit(solution)/shard_map/ppermute | solution.py:60
  26.7 1.0 %fusion.15 = bf16[4,256,512]{2,1,0:T(8,128)(2,1)S(1)} fusion(bf16[1,640,512]{2,1,0:T(8,128)(2,1)S(1)} %bitcast.107, bf16[1,640,512]{2,1,0:T(8,128)(2,1)S(1)} %bitcast.108, bf16[1,640,512]{2,1,0:T(8,128)(2,1)S(1)} %bitcast.109, bf16[1,640,512]{2,1,0:T(8,128)(2,1)S(1)} %bitcast.110, f32[4,640]{1,0:T(4,128)S(1)} %bitcast.111, f32[256,640]{1,0:T(8,128)S(1)} %copy-done.1), kind=kOutput, calls=%fused_computation.16 | convolution fusion | flops 676855808 | bytes 4335616 | tf_op jit(solution)/shard_map/dot_general | solution.py:109
  27.8 0.4 maximum_bitcast_fusion
  28.2 1.3 %fusion.8 = f32[2,512,512]{2,1,0:T(8,128)S(1)} fusion(bf16[1,1024,512]{2,1,0:T(8,128)(2,1)S(1)} %get-tuple-element.9, bf16[1,1024,512]{2,1,0:T(8,128)(2,1)S(1)} %get-tuple-element.6, bf16[1,1024,512]{2,1,0:T(8,128)(2,1)S(1)} %get-tuple-element.10, bf16[1,1024,512]{2,1,0:T(8,128)(2,1)S(1)} %get-tuple-element.5), kind=kOutput, calls=%fused_computation.9 | convolution fusion | flops 1075838976 | bytes 6291456 | tf_op jit(solution)/shard_map/dot_general | solution.py:119
  29.5 1.1 %dynamic-slice_bitcast_fusion = f32[2,32,8,512]{3,2,1,0:T(8,128)} fusion(f32[2,32,2,8,512]{4,3,2,1,0:T(8,128)S(1)} %bitcast.101, s32[]{:T(128)S(6)} %select_n.17), kind=kLoop, calls=%fused_computation.26 | loop fusion | bytes 2097156 | tf_op jit(solution)/shard_map/jit(dynamic_index_in_dim)/squeeze | solution.py:130
  30.6 1.9 %collective-permute-start.5 = (f32[2,32,8,512]{3,2,1,0:T(8,128)}, f32[2,32,8,512]{3,2,1,0:T(8,128)}, u32[]{:S(2)}, u32[]{:S(2)}) collective-permute-start(f32[2,32,8,512]{3,2,1,0:T(8,128)} %dynamic-slice_bitcast_fusion), channel_id=1, source_target_pairs={{0,8},{8,0},{1,9},{9,1},{2,10},{10,2},{3,11},{11,3},{4,12},{12,4},... | collective-permute-start | bytes 3145736 | tf_op jit(solution)/shard_map/ppermute | solution.py:132
  32.5 3.0 %collective-permute-done.5 = f32[2,32,8,512]{3,2,1,0:T(8,128)} collective-permute-done((f32[2,32,8,512]{3,2,1,0:T(8,128)}, f32[2,32,8,512]{3,2,1,0:T(8,128)}, u32[]{:S(2)}, u32[]{:S(2)}) %collective-permute-start.5) | collective-permute-done | bytes 1048608 | tf_op jit(solution)/shard_map/ppermute | solution.py:132
  35.5 2.4 %bitcast_add_fusion = f32[2,32,8,512]{3,2,1,0:T(8,128)} fusion(f32[2,32,8,512]{3,2,1,0:T(8,128)} %collective-permute-done.5, f32[2,32,2,8,512]{4,3,2,1,0:T(8,128)S(1)} %bitcast.102, s32[]{:T(128)S(6)} %select_n.16), kind=kLoop, calls=%fused_computation.25 | loop fusion | flops 262144 | bytes 3145732 | tf_op jit(solution)/shard_map/add | solution.py:132
  37.9 1.6 %reshape.66 = f32[2,32,8,8,64]{4,3,2,1,0:T(8,128)S(1)} reshape(f32[2,32,8,512]{3,2,1,0:T(8,128)} %bitcast_add_fusion) | data formatting | bytes 2097152 | tf_op jit(solution)/shard_map/reshape | solution.py:133
  39.5 1.7 %copy.9 = f32[8,2,32,8,64]{4,3,2,1,0:T(8,128)} copy(f32[8,2,32,8,64]{4,0,3,2,1:T(8,128)S(1)} %bitcast.100) | data formatting | bytes 2097152 | tf_op jit(solution)/shard_map/transpose | solution.py:133
  41.2 1.8 %reshape.67 = f32[8,256,128]{2,1,0:T(8,128)S(1)} reshape(f32[8,2,32,8,64]{4,3,2,1,0:T(8,128)} %copy.9) | data formatting | bytes 2097152 | tf_op jit(solution)/shard_map/reshape | solution.py:134
  43.0 24.0 %all_to_all.10 = f32[8,256,128]{2,1,0:T(8,128)S(1)} all-to-all(f32[8,256,128]{2,1,0:T(8,128)S(1)} %reshape.67), channel_id=1, replica_groups=mesh['y_hi'=4,'z'=8,'core'=2,'x'=4,'y_lo'=2] {'x','y_lo'}, dimensions={0} | all-to-all | bytes 2097152 | tf_op jit(solution)/shard_map/all_to_all | solution.py:135
  67.1 0.1 reshape.68
  67.3 0.1 reshape.69
  67.4 24.9 %all_to_all.11 = f32[32,8,128]{2,1,0:T(8,128)S(1)} all-to-all(f32[32,8,128]{2,1,0:T(8,128)S(1)} %reshape.69), channel_id=1, replica_groups=mesh['y_hi'=4,'z'=8,'core'=2,'x'=4,'y_lo'=2] {'y_hi','z'}, dimensions={0} | all-to-all | bytes 262144 | tf_op jit(solution)/shard_map/all_to_all | solution.py:138
  92.3 0.7 reshape.70
  (31 shorter events, 0.6 us)
Async XLA Ops:
  0.0 21.5 %copy-start = (s32[1,1,3,20]{3,1,2,0:T(1,128)S(1)}, s32[1,1,3,20]{3,1,2,0:T(1,128)}, u32[]{:S(2)}) copy-start(s32[1,1,3,20]{3,1,2,0:T(1,128)} %param.7) | copy-start | bytes 724
  1.4 21.0 %collective-permute-start = (bf16[128,512]{1,0:T(8,128)(2,1)S(1)}, bf16[128,512]{1,0:T(8,128)(2,1)S(1)}, u32[]{:S(2)}, u32[]{:S(2)}) collective-permute-start(bf16[128,512]{1,0:T(8,128)(2,1)S(1)} %get-tuple-element.18), channel_id=1, source_target_pairs={{7,0},{0,1},{1,2},{2,3},{3,4},{4,5},{5,6},{6,7},{15,8},{8,9},{9,10... | collective-permute-start | bytes 393224 | tf_op jit(solution)/shard_map/ppermute | solution.py:60
  5.5 17.0 %collective-permute-start.1 = (bf16[2,128,512]{2,1,0:T(8,128)(2,1)S(1)}, bf16[2,128,512]{2,1,0:T(8,128)(2,1)S(1)}, u32[]{:S(2)}, u32[]{:S(2)}) collective-permute-start(bf16[2,128,512]{2,1,0:T(8,128)(2,1)S(1)} %slice_bitcast_fusion.1), channel_id=1, source_target_pairs={{1,0},{2,1},{3,2},{4,3},{5,4},{6,5},{7,6},{0,7},{9,8},{10,9},{11,1... | collective-permute-start | bytes 786440 | tf_op jit(solution)/shard_map/ppermute | solution.py:60
  9.6 13.0 %collective-permute-start.2 = (bf16[128,512]{1,0:T(8,128)(2,1)S(1)}, bf16[128,512]{1,0:T(8,128)(2,1)S(1)}, u32[]{:S(2)}, u32[]{:S(2)}) collective-permute-start(bf16[128,512]{1,0:T(8,128)(2,1)S(1)} %get-tuple-element.19), channel_id=1, source_target_pairs={{15,0},{8,1},{9,2},{10,3},{11,4},{12,5},{13,6},{14,7},{23,8},{16,9... | collective-permute-start | bytes 393224 | tf_op jit(solution)/shard_map/ppermute | solution.py:60
  15.7 8.0 %collective-permute-start.3 = (bf16[2,128,512]{2,1,0:T(8,128)(2,1)S(1)}, bf16[2,128,512]{2,1,0:T(8,128)(2,1)S(1)}, u32[]{:S(2)}, u32[]{:S(2)}) collective-permute-start(bf16[2,128,512]{2,1,0:T(8,128)(2,1)S(1)} %slice_bitcast_fusion), channel_id=1, source_target_pairs={{8,0},{16,8},{24,16},{32,24},{40,32},{48,40},{56,48},{64,56},{72,6... | collective-permute-start | bytes 786440 | tf_op jit(solution)/shard_map/ppermute | solution.py:60
  19.5 7.2 %collective-permute-start.4 = (bf16[128,512]{1,0:T(8,128)(2,1)S(1)}, bf16[128,512]{1,0:T(8,128)(2,1)S(1)}, u32[]{:S(2)}, u32[]{:S(2)}) collective-permute-start(bf16[128,512]{1,0:T(8,128)(2,1)S(1)} %get-tuple-element.20), channel_id=1, source_target_pairs={{9,0},{10,1},{11,2},{12,3},{13,4},{14,5},{15,6},{8,7},{17,8},{18,9... | collective-permute-start | bytes 393224 | tf_op jit(solution)/shard_map/ppermute | solution.py:60
  22.4 4.3 %copy-start.1 = (f32[256,640]{1,0:T(8,128)S(1)}, f32[256,640]{1,0:T(8,128)}, u32[]{:S(2)}) copy-start(f32[256,640]{1,0:T(8,128)} %constant.37) | copy-start | bytes 1966084
  30.6 4.9 %collective-permute-start.5 = (f32[2,32,8,512]{3,2,1,0:T(8,128)}, f32[2,32,8,512]{3,2,1,0:T(8,128)}, u32[]{:S(2)}, u32[]{:S(2)}) collective-permute-start(f32[2,32,8,512]{3,2,1,0:T(8,128)} %dynamic-slice_bitcast_fusion), channel_id=1, source_target_pairs={{0,8},{8,0},{1,9},{9,1},{2,10},{10,2},{3,11},{11,3},{4,12},{12,4},... | collective-permute-start | bytes 3145736 | tf_op jit(solution)/shard_map/ppermute | solution.py:132

commit v10 on v9

--- a/solution.py
+++ b/solution.py
@@ -124,14 +124,13 @@
     n_ci = group_size(CIRC)
     cols = mode_count // n_ci
     rows = mode_count // (outer * n_core)
-    split = summand.reshape(2, outer, n_core, rows, mode_count)
+    split = summand.reshape(2, outer, n_core, rows, n_ci, cols).transpose(2, 4, 0, 1, 3, 5)
+    split = split.reshape(n_core, n_ci, 2 * outer * rows * cols // 128, 128)
     mine = lax.axis_index("core")
-    keep = lax.dynamic_index_in_dim(split, mine, axis=2, keepdims=False)
-    send = lax.dynamic_index_in_dim(split, n_core - 1 - mine, axis=2, keepdims=False)
+    keep = lax.dynamic_index_in_dim(split, mine, axis=0, keepdims=False)
+    send = lax.dynamic_index_in_dim(split, n_core - 1 - mine, axis=0, keepdims=False)
     pairs = [(k, n_core - 1 - k) for k in range(n_core)]
-    half = keep + lax.ppermute(send, "core", pairs)
-    arranged = half.reshape(2, outer, rows, n_ci, cols).transpose(3, 0, 1, 2, 4)
-    arranged = arranged.reshape(n_ci, 2 * outer * rows * cols // 128, 128)
+    arranged = keep + lax.ppermute(send, "core", pairs)
     parts = lax.all_to_all(arranged, CIRC, 0, 0, tiled=True)
     partial_value = parts.sum(axis=0).reshape(2, outer, rows, cols)
     arranged = partial_value.transpose(1, 0, 2, 3).reshape(outer, 2 * rows * cols // 128, 128)

time: 93.9 us -> 97.2 us (1.035)
  local copies, waits for them, and re-layouts: 7.5 us -> 12 us
  other arithmetic: 4.37 us -> 3.27 us
    reshape x2 -> x3, local copies, waits for them, and re-layouts: 3.38 us -> 10.6 us  [the longest x2 7.36 us: body(): summand.reshape(2, outer, n_core, rows, n_ci, cols)]
    transpose x1 -> x0, local copies, waits for them, and re-layouts: 1.71 us -> none  [body(): arranged = half.reshape(2, outer, rows, n_ci, cols).transpose(3, 0, 1, 2, 4)]
    add x1, other arithmetic: 2.43 us -> 1.33 us  [body(): arranged = keep + lax.ppermute(send, 'core', pairs)]
    squeeze x1, local copies, waits for them, and re-layouts: 1.1 us -> 0.08 us  [body(): lax.dynamic_index_in_dim(split, n_core - 1 - mine, axis=0, keepdims=False)]
where the time goes in v10:
time: 97.2 us; the launch traced here: 96.2 us
  blocking collectives  48.9 us (50%)
  starting transfers between devices  21.8 us (22%)
  local copies, waits for them, and re-layouts  12 us (12%)
  waiting for transfers between devices  6.75 us (7%)
  other arithmetic  3.27 us (3%)
  matrix products  2.42 us (2%)
    all_to_all x1, blocking collectives, body(): parts = lax.all_to_all(arranged, AXIAL[:-1], 0, 0, tiled=True)  24.9 us
    all_to_all x1, blocking collectives, body(): parts = lax.all_to_all(arranged, CIRC, 0, 0, tiled=True)  24 us
    ppermute x5, starting transfers between devices, shifted(): return lax.ppermute(block, sum(axes, ()), pairs)  19.9 us
    reshape x2, local copies, waits for them, and re-layouts, body(): summand.reshape(2, outer, n_core, rows, n_ci, cols)  7.36 us
    ppermute x5, waiting for transfers between devices, shifted(): return lax.ppermute(block, sum(axes, ()), pairs)  4 us
    reshape x1, local copies, waits for them, and re-layouts, body(): split = split.reshape(n_core, n_ci, 2 * outer * rows * cols // 128, 128)  3.26 us
    ppermute x1, waiting for transfers between devices, body(): arranged = keep + lax.ppermute(send, 'core', pairs)  2.76 us
  transfers between devices with their start and end apart: 6, of which 3 were waited for; matrix products, arithmetic and copies ran while one was open for 1% of the time, Pallas kernels for 0%

profile of v10, /device:TPU:1, one launch (start us, length us, event | category | flops | bytes accessed | tf_op | source)
XLA Modules:
  0.0 96.2 jit_solution(15517691482866779328)
XLA Ops:
  0.0 1.4 %multiply_convert_fusion.2 = bf16[2,2,128,512]{3,2,1,0:T(8,128)(2,1)S(1)} fusion(f32[2,2,128,512]{3,2,1,0:T(8,128)} %param.5, f32[2,2,128]{2,1,0:T(2,128)} %param.6), kind=kLoop, calls=%fused_computation.28 | loop fusion | flops 524288 | bytes 1574912 | tf_op jit(solution)/shard_map/convert_element_type | solution.py:66
  1.4 4.0 %collective-permute-start = (bf16[128,512]{1,0:T(8,128)(2,1)S(1)}, bf16[128,512]{1,0:T(8,128)(2,1)S(1)}, u32[]{:S(2)}, u32[]{:S(2)}) collective-permute-start(bf16[128,512]{1,0:T(8,128)(2,1)S(1)} %get-tuple-element.18), channel_id=1, source_target_pairs={{7,0},{0,1},{1,2},{2,3},{3,4},{4,5},{5,6},{6,7},{15,8},{8,9},{9,10... | collective-permute-start | bytes 393224 | tf_op jit(solution)/shard_map/ppermute | solution.py:60
  5.5 4.1 %collective-permute-start.1 = (bf16[2,128,512]{2,1,0:T(8,128)(2,1)S(1)}, bf16[2,128,512]{2,1,0:T(8,128)(2,1)S(1)}, u32[]{:S(2)}, u32[]{:S(2)}) collective-permute-start(bf16[2,128,512]{2,1,0:T(8,128)(2,1)S(1)} %slice_bitcast_fusion.1), channel_id=1, source_target_pairs={{1,0},{2,1},{3,2},{4,3},{5,4},{6,5},{7,6},{0,7},{9,8},{10,9},{11,1... | collective-permute-start | bytes 786440 | tf_op jit(solution)/shard_map/ppermute | solution.py:60
  9.6 6.1 %collective-permute-start.2 = (bf16[128,512]{1,0:T(8,128)(2,1)S(1)}, bf16[128,512]{1,0:T(8,128)(2,1)S(1)}, u32[]{:S(2)}, u32[]{:S(2)}) collective-permute-start(bf16[128,512]{1,0:T(8,128)(2,1)S(1)} %get-tuple-element.19), channel_id=1, source_target_pairs={{15,0},{8,1},{9,2},{10,3},{11,4},{12,5},{13,6},{14,7},{23,8},{16,9... | collective-permute-start | bytes 393224 | tf_op jit(solution)/shard_map/ppermute | solution.py:60
  15.7 3.8 %collective-permute-start.3 = (bf16[2,128,512]{2,1,0:T(8,128)(2,1)S(1)}, bf16[2,128,512]{2,1,0:T(8,128)(2,1)S(1)}, u32[]{:S(2)}, u32[]{:S(2)}) collective-permute-start(bf16[2,128,512]{2,1,0:T(8,128)(2,1)S(1)} %slice_bitcast_fusion), channel_id=1, source_target_pairs={{8,0},{16,8},{24,16},{32,24},{40,32},{48,40},{56,48},{64,56},{72,6... | collective-permute-start | bytes 786440 | tf_op jit(solution)/shard_map/ppermute | solution.py:60
  19.5 1.9 %collective-permute-start.4 = (bf16[128,512]{1,0:T(8,128)(2,1)S(1)}, bf16[128,512]{1,0:T(8,128)(2,1)S(1)}, u32[]{:S(2)}, u32[]{:S(2)}) collective-permute-start(bf16[128,512]{1,0:T(8,128)(2,1)S(1)} %get-tuple-element.20), channel_id=1, source_target_pairs={{9,0},{10,1},{11,2},{12,3},{13,4},{14,5},{15,6},{8,7},{17,8},{18,9... | collective-permute-start | bytes 393224 | tf_op jit(solution)/shard_map/ppermute | solution.py:60
  22.2 0.1 fusion.32
  22.6 1.0 %collective-permute-done.3 = bf16[2,128,512]{2,1,0:T(8,128)(2,1)S(1)} collective-permute-done((bf16[2,128,512]{2,1,0:T(8,128)(2,1)S(1)}, bf16[2,128,512]{2,1,0:T(8,128)(2,1)S(1)}, u32[]{:S(2)}, u32[]{:S(2)}) %collective-permute-start.3) | collective-permute-done | bytes 262176 | tf_op jit(solution)/shard_map/ppermute | solution.py:60
  23.7 2.9 %collective-permute-done.4 = bf16[128,512]{1,0:T(8,128)(2,1)S(1)} collective-permute-done((bf16[128,512]{1,0:T(8,128)(2,1)S(1)}, bf16[128,512]{1,0:T(8,128)(2,1)S(1)}, u32[]{:S(2)}, u32[]{:S(2)}) %collective-permute-start.4) | collective-permute-done | bytes 131104 | tf_op jit(solution)/shard_map/ppermute | solution.py:60
  26.7 1.0 %fusion.15 = bf16[4,256,512]{2,1,0:T(8,128)(2,1)S(1)} fusion(bf16[1,640,512]{2,1,0:T(8,128)(2,1)S(1)} %bitcast.104, bf16[1,640,512]{2,1,0:T(8,128)(2,1)S(1)} %bitcast.105, bf16[1,640,512]{2,1,0:T(8,128)(2,1)S(1)} %bitcast.106, bf16[1,640,512]{2,1,0:T(8,128)(2,1)S(1)} %bitcast.107, f32[4,640]{1,0:T(4,128)S(1)} %bitcast.108, f32[256,640]{1,0:T(8,128)S(1)} %copy-done.1), kind=kOutput, calls=%fused_computation.17 | convolution fusion | flops 676855808 | bytes 4335616 | tf_op jit(solution)/shard_map/dot_general | solution.py:109
  27.8 0.4 maximum_bitcast_fusion
  28.2 1.3 %fusion.8 = f32[2,512,512]{2,1,0:T(8,128)S(1)} fusion(bf16[1,1024,512]{2,1,0:T(8,128)(2,1)S(1)} %get-tuple-element.9, bf16[1,1024,512]{2,1,0:T(8,128)(2,1)S(1)} %get-tuple-element.6, bf16[1,1024,512]{2,1,0:T(8,128)(2,1)S(1)} %get-tuple-element.10, bf16[1,1024,512]{2,1,0:T(8,128)(2,1)S(1)} %get-tuple-element.5), kind=kOutput, calls=%fused_computation.10 | convolution fusion | flops 1075838976 | bytes 6291456 | tf_op jit(solution)/shard_map/dot_general | solution.py:119
  29.5 2.4 %reshape.62 = f32[2,32,2,8,8,64]{5,4,3,2,1,0:T(8,128)} reshape(f32[2,512,512]{2,1,0:T(8,128)S(1)} %fusion.8) | data formatting | bytes 4194304 | tf_op jit(solution)/shard_map/reshape | solution.py:127
  31.9 5.0 %copy.16 = f32[2,32,2,8,8,64]{5,3,1,0,4,2:T(8,128)} copy(f32[2,32,2,8,8,64]{5,4,3,2,1,0:T(8,128)} %reshape.62) | data formatting | bytes 4194304 | tf_op jit(solution)/shard_map/reshape | solution.py:127
  36.9 3.3 %reshape.63 = f32[2,8,256,128]{3,2,1,0:T(8,128)S(1)} reshape(f32[2,8,2,32,8,64]{5,4,3,2,1,0:T(8,128)} %bitcast.99) | data formatting | bytes 4194304 | tf_op jit(solution)/shard_map/reshape | solution.py:128
  40.1 0.1 dynamic-slice_bitcast_fusion
  40.2 1.9 %collective-permute-start.5 = (f32[8,256,128]{2,1,0:T(8,128)S(1)}, f32[8,256,128]{2,1,0:T(8,128)}, u32[]{:S(2)}, u32[]{:S(2)}) collective-permute-start(f32[8,256,128]{2,1,0:T(8,128)S(1)} %dynamic-slice_bitcast_fusion), channel_id=1, source_target_pairs={{0,8},{8,0},{1,9},{9,1},{2,10},{10,2},{3,11},{11,3},{4,12},{12,4},... | collective-permute-start | bytes 3145736 | tf_op jit(solution)/shard_map/ppermute | solution.py:133
  42.2 2.8 %collective-permute-done.5 = f32[8,256,128]{2,1,0:T(8,128)} collective-permute-done((f32[8,256,128]{2,1,0:T(8,128)S(1)}, f32[8,256,128]{2,1,0:T(8,128)}, u32[]{:S(2)}, u32[]{:S(2)}) %collective-permute-start.5) | collective-permute-done | bytes 1048608 | tf_op jit(solution)/shard_map/ppermute | solution.py:133
  44.9 1.3 %bitcast_add_fusion = f32[8,256,128]{2,1,0:T(8,128)S(1)} fusion(f32[8,256,128]{2,1,0:T(8,128)} %collective-permute-done.5, f32[2,8,256,128]{3,2,1,0:T(8,128)S(1)} %reshape.63, s32[]{:T(128)S(6)} %select_n.16), kind=kLoop, calls=%fused_computation.26 | loop fusion | flops 262144 | bytes 3145732 | tf_op jit(solution)/shard_map/add | solution.py:133
  46.2 24.0 %all_to_all.10 = f32[8,256,128]{2,1,0:T(8,128)S(1)} all-to-all(f32[8,256,128]{2,1,0:T(8,128)S(1)} %bitcast_add_fusion), channel_id=1, replica_groups=mesh['y_hi'=4,'z'=8,'core'=2,'x'=4,'y_lo'=2] {'x','y_lo'}, dimensions={0} | all-to-all | bytes 2097152 | tf_op jit(solution)/shard_map/all_to_all | solution.py:134
  70.3 0.1 reshape.64
  70.5 0.1 reshape.65
  70.6 24.9 %all_to_all.11 = f32[32,8,128]{2,1,0:T(8,128)S(1)} all-to-all(f32[32,8,128]{2,1,0:T(8,128)S(1)} %reshape.65), channel_id=1, replica_groups=mesh['y_hi'=4,'z'=8,'core'=2,'x'=4,'y_lo'=2] {'y_hi','z'}, dimensions={0} | all-to-all | bytes 262144 | tf_op jit(solution)/shard_map/all_to_all | solution.py:137
  95.5 0.7 reshape.66
  (31 shorter events, 0.6 us)
Async XLA Ops:
  0.0 21.5 %copy-start = (s32[1,1,3,20]{3,1,2,0:T(1,128)S(1)}, s32[1,1,3,20]{3,1,2,0:T(1,128)}, u32[]{:S(2)}) copy-start(s32[1,1,3,20]{3,1,2,0:T(1,128)} %param.7) | copy-start | bytes 724
  1.4 21.0 %collective-permute-start = (bf16[128,512]{1,0:T(8,128)(2,1)S(1)}, bf16[128,512]{1,0:T(8,128)(2,1)S(1)}, u32[]{:S(2)}, u32[]{:S(2)}) collective-permute-start(bf16[128,512]{1,0:T(8,128)(2,1)S(1)} %get-tuple-element.18), channel_id=1, source_target_pairs={{7,0},{0,1},{1,2},{2,3},{3,4},{4,5},{5,6},{6,7},{15,8},{8,9},{9,10... | collective-permute-start | bytes 393224 | tf_op jit(solution)/shard_map/ppermute | solution.py:60
  5.5 17.0 %collective-permute-start.1 = (bf16[2,128,512]{2,1,0:T(8,128)(2,1)S(1)}, bf16[2,128,512]{2,1,0:T(8,128)(2,1)S(1)}, u32[]{:S(2)}, u32[]{:S(2)}) collective-permute-start(bf16[2,128,512]{2,1,0:T(8,128)(2,1)S(1)} %slice_bitcast_fusion.1), channel_id=1, source_target_pairs={{1,0},{2,1},{3,2},{4,3},{5,4},{6,5},{7,6},{0,7},{9,8},{10,9},{11,1... | collective-permute-start | bytes 786440 | tf_op jit(solution)/shard_map/ppermute | solution.py:60
  9.6 13.0 %collective-permute-start.2 = (bf16[128,512]{1,0:T(8,128)(2,1)S(1)}, bf16[128,512]{1,0:T(8,128)(2,1)S(1)}, u32[]{:S(2)}, u32[]{:S(2)}) collective-permute-start(bf16[128,512]{1,0:T(8,128)(2,1)S(1)} %get-tuple-element.19), channel_id=1, source_target_pairs={{15,0},{8,1},{9,2},{10,3},{11,4},{12,5},{13,6},{14,7},{23,8},{16,9... | collective-permute-start | bytes 393224 | tf_op jit(solution)/shard_map/ppermute | solution.py:60
  15.7 8.0 %collective-permute-start.3 = (bf16[2,128,512]{2,1,0:T(8,128)(2,1)S(1)}, bf16[2,128,512]{2,1,0:T(8,128)(2,1)S(1)}, u32[]{:S(2)}, u32[]{:S(2)}) collective-permute-start(bf16[2,128,512]{2,1,0:T(8,128)(2,1)S(1)} %slice_bitcast_fusion), channel_id=1, source_target_pairs={{8,0},{16,8},{24,16},{32,24},{40,32},{48,40},{56,48},{64,56},{72,6... | collective-permute-start | bytes 786440 | tf_op jit(solution)/shard_map/ppermute | solution.py:60
  19.5 7.2 %collective-permute-start.4 = (bf16[128,512]{1,0:T(8,128)(2,1)S(1)}, bf16[128,512]{1,0:T(8,128)(2,1)S(1)}, u32[]{:S(2)}, u32[]{:S(2)}) collective-permute-start(bf16[128,512]{1,0:T(8,128)(2,1)S(1)} %get-tuple-element.20), channel_id=1, source_target_pairs={{9,0},{10,1},{11,2},{12,3},{13,4},{14,5},{15,6},{8,7},{17,8},{18,9... | collective-permute-start | bytes 393224 | tf_op jit(solution)/shard_map/ppermute | solution.py:60
  22.4 4.3 %copy-start.1 = (f32[256,640]{1,0:T(8,128)S(1)}, f32[256,640]{1,0:T(8,128)}, u32[]{:S(2)}) copy-start(f32[256,640]{1,0:T(8,128)} %constant.37) | copy-start | bytes 1966084
  40.2 4.7 %collective-permute-start.5 = (f32[8,256,128]{2,1,0:T(8,128)S(1)}, f32[8,256,128]{2,1,0:T(8,128)}, u32[]{:S(2)}, u32[]{:S(2)}) collective-permute-start(f32[8,256,128]{2,1,0:T(8,128)S(1)} %dynamic-slice_bitcast_fusion), channel_id=1, source_target_pairs={{0,8},{8,0},{1,9},{9,1},{2,10},{10,2},{3,11},{11,3},{4,12},{12,4},... | collective-permute-start | bytes 3145736 | tf_op jit(solution)/shard_map/ppermute | solution.py:133

commit v11 on v7

--- a/solution.py
+++ b/solution.py
@@ -104,10 +104,12 @@
     rounded = row_sums.astype(jnp.bfloat16).reshape(block_count, 2, patch_count, mode_count)
     rounded = jnp.transpose(rounded, (1, 0, 2, 3)).reshape(2, block_count * patch_count, mode_count)
     local = weighted.reshape(block_count * patch_count, mode_count)
-    first = jnp.stack([jnp.concatenate([local, rounded[q]], axis=0) for q in range(2)])
-    second = jnp.stack(
-        [jnp.concatenate([rounded[0], local], axis=0), jnp.concatenate([rounded[1], -local], axis=0)]
+    shared = jnp.stack(
+        [jnp.concatenate([local, rounded[0], local], axis=0), jnp.concatenate([local, rounded[1], -local], axis=0)]
     )
+    span = 2 * block_count * patch_count
+    first = shared[:, :span]
+    second = shared[:, block_count * patch_count :]
     summand = lax.dot_general(
         first, second, (((1,), (1,)), ((0,), (0,))), preferred_element_type=jnp.float32
     )

time: 93.9 us -> 93.6 us (level)
  no operation moved by 1% of the time
where the time goes in v11:
time: 93.6 us; the launch traced here: 93.1 us
  blocking collectives  60.7 us (65%)
  starting transfers between devices  19.9 us (21%)
  local copies, waits for them, and re-layouts  5.6 us (6%)
  matrix products  3.5 us (4%)
  other arithmetic  1.96 us (2%)
    all_to_all x1, blocking collectives, body(): lax.all_to_all(summand.reshape(2, mode_count, n_ci, cols), 'circ', 2, 0,...  35.4 us
    all_to_all x1, blocking collectives, body(): parts = lax.all_to_all(arranged, 'axial', 0, 0, tiled=True)  25.3 us
    ppermute x5, starting transfers between devices, shifted(): return lax.ppermute(block, axes if len(axes) > 1 else axes[0], pairs)  19.9 us
    unnamed x14, local copies, waits for them, and re-layouts  2.81 us
    dot_general x1, matrix products, body(): lax.dot_general(lhs, columns, (((2,), (1,)), ((0,), (0,))), preferred_ele...  2.1 us
  transfers between devices with their start and end apart: 5, of which 1 were waited for; matrix products, arithmetic and copies ran while one was open for 4% of the time, Pallas kernels for 0%

profile of v11, /device:TPU:1, one launch (start us, length us, event | category | flops | bytes accessed | tf_op | source)
XLA Modules:
  0.0 93.1 jit_solution(6659068098812734834)
XLA Ops:
  0.0 1.4 %multiply_convert_fusion.2 = bf16[2,2,128,512]{3,2,1,0:T(8,128)(2,1)S(1)} fusion(f32[2,2,128,512]{3,2,1,0:T(8,128)} %param.5, f32[2,2,128]{2,1,0:T(2,128)} %param.6), kind=kLoop, calls=%fused_computation.24 | loop fusion | flops 524288 | bytes 1574912 | tf_op jit(solution)/shard_map/convert_element_type | solution.py:58
  1.4 4.0 %collective-permute-start = (bf16[128,512]{1,0:T(8,128)(2,1)S(1)}, bf16[128,512]{1,0:T(8,128)(2,1)S(1)}, u32[]{:S(2)}, u32[]{:S(2)}) collective-permute-start(bf16[128,512]{1,0:T(8,128)(2,1)S(1)} %get-tuple-element.16), channel_id=1, source_target_pairs={{7,0},{0,1},{1,2},{2,3},{3,4},{4,5},{5,6},{6,7},{15,8},{8,9},{9,10... | collective-permute-start | bytes 393224 | tf_op jit(solution)/shard_map/ppermute | solution.py:52
  5.5 4.1 %collective-permute-start.1 = (bf16[2,128,512]{2,1,0:T(8,128)(2,1)S(1)}, bf16[2,128,512]{2,1,0:T(8,128)(2,1)S(1)}, u32[]{:S(2)}, u32[]{:S(2)}) collective-permute-start(bf16[2,128,512]{2,1,0:T(8,128)(2,1)S(1)} %slice_bitcast_fusion.1), channel_id=1, source_target_pairs={{1,0},{2,1},{3,2},{4,3},{5,4},{6,5},{7,6},{0,7},{9,8},{10,9},{11,1... | collective-permute-start | bytes 786440 | tf_op jit(solution)/shard_map/ppermute | solution.py:52
  9.6 6.1 %collective-permute-start.2 = (bf16[128,512]{1,0:T(8,128)(2,1)S(1)}, bf16[128,512]{1,0:T(8,128)(2,1)S(1)}, u32[]{:S(2)}, u32[]{:S(2)}) collective-permute-start(bf16[128,512]{1,0:T(8,128)(2,1)S(1)} %get-tuple-element.17), channel_id=1, source_target_pairs={{15,0},{8,1},{9,2},{10,3},{11,4},{12,5},{13,6},{14,7},{23,8},{16,9... | collective-permute-start | bytes 393224 | tf_op jit(solution)/shard_map/ppermute | solution.py:52
  15.7 3.8 %collective-permute-start.3 = (bf16[2,128,512]{2,1,0:T(8,128)(2,1)S(1)}, bf16[2,128,512]{2,1,0:T(8,128)(2,1)S(1)}, u32[]{:S(2)}, u32[]{:S(2)}) collective-permute-start(bf16[2,128,512]{2,1,0:T(8,128)(2,1)S(1)} %slice_bitcast_fusion), channel_id=1, source_target_pairs={{8,0},{16,8},{24,16},{32,24},{40,32},{48,40},{56,48},{64,56},{72,6... | collective-permute-start | bytes 786440 | tf_op jit(solution)/shard_map/ppermute | solution.py:52
  19.5 1.9 %collective-permute-start.4 = (bf16[128,512]{1,0:T(8,128)(2,1)S(1)}, bf16[128,512]{1,0:T(8,128)(2,1)S(1)}, u32[]{:S(2)}, u32[]{:S(2)}) collective-permute-start(bf16[128,512]{1,0:T(8,128)(2,1)S(1)} %get-tuple-element.18), channel_id=1, source_target_pairs={{9,0},{10,1},{11,2},{12,3},{13,4},{14,5},{15,6},{8,7},{17,8},{18,9... | collective-permute-start | bytes 393224 | tf_op jit(solution)/shard_map/ppermute | solution.py:52
  21.4 0.7 constant_dynamic-update-slice_fusion.3
  22.9 0.2 copy.29
  23.3 0.7 constant_dynamic-update-slice_fusion.2
  24.0 0.7 constant_dynamic-update-slice_fusion.1
  24.6 0.7 fusion.30
  25.3 0.7 constant_dynamic-update-slice_fusion
  26.1 0.5 collective-permute-done.4
  26.7 2.1 %fusion.16 = bf16[4,256,512]{2,1,0:T(8,128)(2,1)S(1)} fusion(bf16[1,640,512]{2,1,0:T(8,128)(2,1)S(1)} %bitcast.93, bf16[1,640,512]{2,1,0:T(8,128)(2,1)S(1)} %bitcast.94, bf16[1,640,512]{2,1,0:T(8,128)(2,1)S(1)} %bitcast.95, bf16[1,640,512]{2,1,0:T(8,128)(2,1)} %bitcast.96, f32[4,640]{1,0:T(4,128)S(1)} %bitcast.97, f32[256,640]{1,0:T(8,128)S(1)} %copy-done.1), kind=kOutput, calls=%fused_computation.21 | convolution fusion | flops 676855808 | bytes 4335616 | tf_op jit(solution)/shard_map/dot_general | solution.py:101
  28.9 0.2 copy.40
  29.1 0.2 copy.41
  29.4 0.2 fusion.15
  29.6 1.3 %fusion.9 = f32[2,512,512]{1,2,0:T(8,128)S(1)} fusion(bf16[1,1536,512]{1,2,0:T(8,128)(2,1)S(1)} %get-tuple-element.8, bf16[1,1536,512]{1,2,0:T(8,128)(2,1)S(1)} %get-tuple-element.7), kind=kOutput, calls=%fused_computation.12 | convolution fusion | flops 1078984704 | bytes 8388608 | tf_op jit(solution)/shard_map/dot_general | solution.py:113
  30.9 0.2 copy.35
  31.1 35.4 %all_to_all.14 = f32[2,512,8,64]{1,3,0,2:T(8,128)S(1)} all-to-all(f32[2,512,8,64]{1,3,0,2:T(8,128)S(1)} %copy.35), channel_id=1, replica_groups=mesh['axial'=64,'circ'=8] {'circ'}, dimensions={2} | all-to-all | bytes 4194304 | tf_op jit(solution)/shard_map/all_to_all | solution.py:120
  66.4 0.2 reduce_sum.18
  66.6 0.2 copy.37
  67.0 25.3 %all_to_all.15 = f32[64,8,128]{2,1,0:T(8,128)S(1)} all-to-all(f32[64,8,128]{2,1,0:T(8,128)S(1)} %reshape.63), channel_id=1, replica_groups=mesh['axial'=64,'circ'=8] {'axial'}, dimensions={0} | all-to-all | bytes 524288 | tf_op jit(solution)/shard_map/all_to_all | solution.py:126
  92.4 0.7 reshape.64
  (28 shorter events, 0.8 us)
Async XLA Ops:
  0.0 22.1 %copy-start = (s32[1,1,3,20]{3,1,2,0:T(1,128)S(1)}, s32[1,1,3,20]{3,1,2,0:T(1,128)}, u32[]{:S(2)}) copy-start(s32[1,1,3,20]{3,1,2,0:T(1,128)} %param.7) | copy-start | bytes 724
  1.4 22.5 %collective-permute-start = (bf16[128,512]{1,0:T(8,128)(2,1)S(1)}, bf16[128,512]{1,0:T(8,128)(2,1)S(1)}, u32[]{:S(2)}, u32[]{:S(2)}) collective-permute-start(bf16[128,512]{1,0:T(8,128)(2,1)S(1)} %get-tuple-element.16), channel_id=1, source_target_pairs={{7,0},{0,1},{1,2},{2,3},{3,4},{4,5},{5,6},{6,7},{15,8},{8,9},{9,10... | collective-permute-start | bytes 393224 | tf_op jit(solution)/shard_map/ppermute | solution.py:52
  5.5 19.8 %collective-permute-start.1 = (bf16[2,128,512]{2,1,0:T(8,128)(2,1)S(1)}, bf16[2,128,512]{2,1,0:T(8,128)(2,1)S(1)}, u32[]{:S(2)}, u32[]{:S(2)}) collective-permute-start(bf16[2,128,512]{2,1,0:T(8,128)(2,1)S(1)} %slice_bitcast_fusion.1), channel_id=1, source_target_pairs={{1,0},{2,1},{3,2},{4,3},{5,4},{6,5},{7,6},{0,7},{9,8},{10,9},{11,1... | collective-permute-start | bytes 786440 | tf_op jit(solution)/shard_map/ppermute | solution.py:52
  9.6 16.4 %collective-permute-start.2 = (bf16[128,512]{1,0:T(8,128)(2,1)S(1)}, bf16[128,512]{1,0:T(8,128)(2,1)S(1)}, u32[]{:S(2)}, u32[]{:S(2)}) collective-permute-start(bf16[128,512]{1,0:T(8,128)(2,1)S(1)} %get-tuple-element.17), channel_id=1, source_target_pairs={{15,0},{8,1},{9,2},{10,3},{11,4},{12,5},{13,6},{14,7},{23,8},{16,9... | collective-permute-start | bytes 393224 | tf_op jit(solution)/shard_map/ppermute | solution.py:52
  15.7 10.4 %collective-permute-start.3 = (bf16[2,128,512]{2,1,0:T(8,128)(2,1)S(1)}, bf16[2,128,512]{2,1,0:T(8,128)(2,1)S(1)}, u32[]{:S(2)}, u32[]{:S(2)}) collective-permute-start(bf16[2,128,512]{2,1,0:T(8,128)(2,1)S(1)} %slice_bitcast_fusion), channel_id=1, source_target_pairs={{8,0},{16,8},{24,16},{32,24},{40,32},{48,40},{56,48},{64,56},{72,6... | collective-permute-start | bytes 786440 | tf_op jit(solution)/shard_map/ppermute | solution.py:52
  19.5 7.2 %collective-permute-start.4 = (bf16[128,512]{1,0:T(8,128)(2,1)S(1)}, bf16[128,512]{1,0:T(8,128)(2,1)S(1)}, u32[]{:S(2)}, u32[]{:S(2)}) collective-permute-start(bf16[128,512]{1,0:T(8,128)(2,1)S(1)} %get-tuple-element.18), channel_id=1, source_target_pairs={{9,0},{10,1},{11,2},{12,3},{13,4},{14,5},{15,6},{8,7},{17,8},{18,9... | collective-permute-start | bytes 393224 | tf_op jit(solution)/shard_map/ppermute | solution.py:52
  23.3 3.4 %copy-start.1 = (f32[256,640]{1,0:T(8,128)S(1)}, f32[256,640]{1,0:T(8,128)}, u32[]{:S(2)}) copy-start(f32[256,640]{1,0:T(8,128)} %constant.21) | copy-start | bytes 1966084
